TPU v7x, 32 devices: a whole 2x2x4 slice. The times are simulated.
32 devices in a mesh: cell: 4 (over y, x), blk: 8 (over z, core).
Axes of the slice: x: 2, y: 2, z: 4, core: 2. Of those that a mesh axis runs over, the one named last changes fastest.
Arguments:
- codes: bfloat16 [16384, 128], P(('cell', 'blk')), may hold values from -60 to 60
- scales: float32 [16384], P(('cell', 'blk')), may hold values from 0.5 to 2
- coarse_ids: int32 [16384], P(('cell', 'blk')), may hold values from 0 to 3, as said below
- centroids: bfloat16 [32768, 128], P(('cell', 'blk')), may hold values from -6 to 6
Outputs:
- reconstruction: bfloat16 [16384, 128], P(('cell', 'blk'))
- residual: bfloat16 [16384, 128], P(('cell', 'blk'))
Inputs may be any that keep to these rules, and one draw needn't show every extreme that they name: `coarse_ids`: on every device, the number of its 512 rows that name partition g is the same for all devices; at most 256 rows of one device name one partition, and one partition is named by exactly 256 rows of every device.
All inputs are finite; a program needn't handle non-finite values.
Results may differ from a plain program's by a relative error of at most 0.006.
Values may be sent and summed in bfloat16 or wider, within the bound.
No kernel may reach another device: no remote copies, remote signals or barrier semaphores. Data moves between devices by JAX's collectives and lax.ppermute only.
A program may use at most 256 MiB of HBM per device.

v0:
```python
import functools
import math

import jax
import jax.numpy as jnp
from jax import lax
from jax.experimental import pallas as pl
from jax.experimental.pallas import tpu as pltpu
from jax.sharding import PartitionSpec as P


def _soft_kernel(*refs, chunk, beta, merge, final):
    if not merge and final:
        q_ref, c_ref, o_ref, m_sc, l_sc, acc_sc, s_sc = refs
    elif merge:
        q_ref, c_ref, pm_ref, pl_ref, pacc_ref, o_ref, m_sc, l_sc, acc_sc, s_sc = refs
    else:
        q_ref, c_ref, om_ref, ol_ref, oacc_ref, m_sc, l_sc, acc_sc, s_sc = refs
    n_chunks = c_ref.shape[0] // chunk
    lanes = m_sc.shape[1]
    q = q_ref[...]
    m_sc[...] = jnp.full(m_sc.shape, -jnp.inf, jnp.float32)

    @pl.loop(0, n_chunks)
    def _(i):
        cols = pl.ds(pl.multiple_of(i * chunk, chunk), chunk)
        s = lax.dot_general(
            q, c_ref[cols, :], (((1,), (1,)), ((), ())), preferred_element_type=jnp.float32
        ) * beta
        s_sc[:, cols] = s
        m = m_sc[...]
        for j in range(chunk // lanes):
            m = jnp.maximum(m, s[:, j * lanes:(j + 1) * lanes])
        m_sc[...] = m

    top = jnp.max(m_sc[...], axis=1, keepdims=True)
    if merge:
        top = jnp.maximum(top, pm_ref[...])
    l_sc[...] = jnp.zeros(l_sc.shape, jnp.float32)
    acc_sc[...] = jnp.zeros(acc_sc.shape, jnp.float32)

    @pl.loop(0, n_chunks)
    def _(i):
        cols = pl.ds(pl.multiple_of(i * chunk, chunk), chunk)
        w = jnp.exp(s_sc[:, cols] - top).astype(jnp.bfloat16)
        wf = w.astype(jnp.float32)
        l = l_sc[...]
        for j in range(chunk // lanes):
            l = l + wf[:, j * lanes:(j + 1) * lanes]
        l_sc[...] = l
        acc_sc[...] += jnp.dot(w, c_ref[cols, :], preferred_element_type=jnp.float32)

    total = jnp.sum(l_sc[...], axis=1, keepdims=True)
    if final and not merge:
        o_ref[...] = (acc_sc[...] / total).astype(o_ref.dtype)
    elif merge:
        scale = jnp.exp(pm_ref[...] - top)
        total = total + pl_ref[...] * scale
        numer = acc_sc[...] + pacc_ref[...] * scale
        o_ref[...] = (numer / total).astype(o_ref.dtype)
    else:
        om_ref[...] = top
        ol_ref[...] = total
        oacc_ref[...] = acc_sc[...]


def soft_part(queries, cents, prior=None, final=False):
    slots, width = queries.shape
    n_cent = cents.shape[0]
    chunk = min(4096, n_cent)
    tq = slots
    while tq * n_cent * 4 > (32 << 20) and tq % 16 == 0:
        tq //= 2
    vmem = 4 * tq * n_cent + 2 * 2 * n_cent * width + 16 * tq * width * 4 + (8 << 20)
    rows = pl.BlockSpec((tq, width), lambda i: (i, 0))
    col = pl.BlockSpec((tq, 1), lambda i: (i, 0))
    in_specs = [rows, pl.BlockSpec((n_cent, width), lambda i: (0, 0))]
    stats = [
        jax.ShapeDtypeStruct((slots, 1), jnp.float32),
        jax.ShapeDtypeStruct((slots, 1), jnp.float32),
        jax.ShapeDtypeStruct((slots, width), jnp.float32),
    ]
    if prior is None and final:
        out_shape = jax.ShapeDtypeStruct((slots, width), jnp.bfloat16)
        out_specs, args = rows, (queries, cents)
    elif prior is None:
        out_shape, out_specs, args = stats, [col, col, rows], (queries, cents)
    else:
        in_specs += [col, col, rows]
        out_shape = jax.ShapeDtypeStruct((slots, width), jnp.bfloat16)
        out_specs, args = rows, (queries, cents) + tuple(prior)
    return pl.pallas_call(
        functools.partial(
            _soft_kernel,
            chunk=chunk,
            beta=1.0 / math.sqrt(width),
            merge=prior is not None,
            final=final or prior is not None,
        ),
        out_shape=out_shape,
        grid=(slots // tq,),
        in_specs=in_specs,
        out_specs=out_specs,
        scratch_shapes=[
            pltpu.VMEM((tq, 128), jnp.float32),
            pltpu.VMEM((tq, 128), jnp.float32),
            pltpu.VMEM((tq, width), jnp.float32),
            pltpu.VMEM((tq, n_cent), jnp.float32),
        ],
        compiler_params=pltpu.CompilerParams(vmem_limit_bytes=min(vmem, 60 << 20)),
        cost_estimate=pl.CostEstimate(
            flops=2 * 2 * slots * n_cent * width,
            transcendentals=slots * n_cent,
            bytes_accessed=2 * (2 * slots * width + n_cent * width),
        ),
    )(*args)


def _shift(x, axis, n, d):
    return lax.ppermute(x, axis, [(i, (i + d) % n) for i in range(n)])


def _gather_partition(centroids):
    n_blk = lax.axis_size("blk")
    n_chip = n_blk // 2
    pieces = [centroids]
    for d in range(1, n_chip):
        pairs = [(k * 2 + c, ((k + d) % n_chip) * 2 + c) for k in range(n_chip) for c in range(2)]
        pieces.append(lax.ppermute(centroids, "blk", pairs))
    swap = [(b, b ^ 1) for b in range(n_blk)]
    swapped = [lax.ppermute(p, "blk", swap) for p in pieces]
    return jnp.concatenate(pieces + swapped, axis=0)


def _local(codes, scales, coarse_ids, centroids):
    rows_dev = codes.shape[0]
    width = codes.shape[1]
    loops = lax.axis_size("cell")
    cap = 2 * rows_dev // loops
    me = lax.axis_index("cell")
    dequant = (codes.astype(jnp.float32) * scales[:, None]).astype(jnp.bfloat16)
    onehot = (coarse_ids[:, None] == jnp.arange(loops, dtype=jnp.int32)[None, :]).astype(jnp.int32)
    ranks = jnp.sum(jnp.cumsum(onehot, axis=0) * onehot, axis=1) - 1
    slots = ((coarse_ids - me) % loops) * cap + ranks
    outgoing = jnp.zeros((loops * cap, width), jnp.bfloat16).at[slots].set(dequant)
    outgoing = outgoing.reshape(loops, cap, width)
    part = _gather_partition(centroids)
    arrived = [outgoing[0]] + [_shift(outgoing[d], "cell", loops, d) for d in range(1, loops)]
    first = soft_part(jnp.concatenate(arrived[1:], axis=0), part, final=True)
    ret = {d: _shift(first[(d - 1) * cap:d * cap], "cell", loops, -d) for d in range(1, loops)}
    ret[0] = soft_part(arrived[0], part, final=True)
    mine = jnp.concatenate([ret[d] for d in range(loops)], axis=0)[slots]
    residual = (dequant.astype(jnp.float32) - mine.astype(jnp.float32)).astype(jnp.bfloat16)
    return (mine, residual)


def solution(mesh):
    rows = P(("cell", "blk"), None)
    in_specs = (rows, P(("cell", "blk")), P(("cell", "blk")), rows)
    out_specs = (rows, rows)
    return jax.shard_map(_local, mesh=mesh, in_specs=in_specs, out_specs=out_specs, check_vma=False)
```

profile of v0, /device:TPU:0, one launch (start us, length us, event | category | flops | bytes accessed | tf_op | source)
XLA Modules:
  0.0 50.3 jit_solution(16031197461436456062)
XLA Ops:
  0.6 3.1 %collective-permute-start = (bf16[1024,128]{1,0:T(8,128)(2,1)}, bf16[1024,128]{1,0:T(8,128)(2,1)S(1)}, u32[]{:S(2)}, u32[]{:S(2)}) collective-permute-start(bf16[1024,128]{1,0:T(8,128)(2,1)} %param.7), channel_id=1, source_target_pairs={{0,2},{1,3},{2,4},{3,5},{4,6},{5,7},{6,0},{7,1},{8,10},{9,11},{10,... | collective-permute-start | bytes 786440 | tf_op jit(solution)/shard_map/ppermute | solution.py:129
  3.7 2.6 %collective-permute-start.1 = (bf16[1024,128]{1,0:T(8,128)(2,1)}, bf16[1024,128]{1,0:T(8,128)(2,1)S(1)}, u32[]{:S(2)}, u32[]{:S(2)}) collective-permute-start(bf16[1024,128]{1,0:T(8,128)(2,1)} %param.7), channel_id=1, source_target_pairs={{0,4},{1,5},{2,6},{3,7},{4,0},{5,1},{6,2},{7,3},{8,12},{9,13},{10,... | collective-permute-start | bytes 786440 | tf_op jit(solution)/shard_map/ppermute | solution.py:129
  6.3 0.7 %fusion.4 = s32[4,4,128]{2,1,0:T(4,128)S(1)} fusion(s32[4,128]{1,0:T(4,128)} %bitcast.16), kind=kLoop, calls=%fused_computation.23 | loop fusion | flops 4096 | bytes 10240 | tf_op jit(solution)/shard_map/convert_element_type | solution.py:142
  7.0 1.2 %reduce-window.6 = s32[4,4,128]{2,1,0:T(4,128)S(1)} reduce-window(s32[4,4,128]{2,1,0:T(4,128)S(1)} %fusion.4, s32[]{:T(128)} %constant.29.clone.1), window={size=1x1x128 pad=0_0x0_0x127_0}, to_apply=%region_0.0 | reduce-window | flops 260096 | bytes 16388 | tf_op jit(solution)/shard_map/reduce-window
  8.2 0.2 slice_reduce_fusion
  8.4 0.2 reduce-window.9
  8.6 0.1 add_bitcast_fusion
  8.7 0.7 %fusion.3 = s32[512]{0:T(512)S(1)} fusion(s32[1,4,4,128]{3,2,1,0:T(4,128)S(1)} %add_bitcast_fusion, s32[512]{0:T(512)} %param.6), kind=kLoop, calls=%fused_computation.18 | loop fusion | flops 5632 | bytes 12288 | tf_op jit(solution)/shard_map/reduce_sum | solution.py:143
  9.4 0.7 %compare_select_fusion = s32[512]{0:T(512)S(1)} fusion(s32[512]{0:T(512)S(1)} %fusion.3, s32[512]{0:T(512)} %param.6, s32[]{:T(128)S(6)} %axis_index.15), kind=kLoop, calls=%fused_computation.24 | loop fusion | flops 9216 | bytes 6148 | tf_op jit(solution)/shard_map/select_n | solution.py:145
  10.1 2.3 %scatter_custom_fusion = bf16[1024,128]{1,0:T(8,128)(2,1)S(1)} fusion(s32[512]{0:T(512)S(1)} %compare_select_fusion, bf16[]{:T(256)} %constant.27.clone.1, bf16[512,128]{1,0:T(8,128)(2,1)} %param.4, f32[512]{0:T(512)} %param.5), kind=kCustom, calls=%fused_computation.6 | custom fusion | flops 196608 | bytes 395266 | tf_op jit(solution)/shard_map/scatter | solution.py:145
  12.4 1.5 %collective-permute-start.7 = (bf16[256,128]{1,0:T(8,128)(2,1)S(1)}, bf16[256,128]{1,0:T(8,128)(2,1)S(1)}, u32[]{:S(2)}, u32[]{:S(2)}) collective-permute-start(bf16[256,128]{1,0:T(8,128)(2,1)S(1)} %get-tuple-element.5), channel_id=1, source_target_pairs={{0,8},{8,16},{16,24},{24,0},{1,9},{9,17},{17,25},{25,1},{2,10},{10... | collective-permute-start | bytes 196616 | tf_op jit(solution)/shard_map/ppermute | solution.py:120
  14.0 1.5 %collective-permute-start.8 = (bf16[256,128]{1,0:T(8,128)(2,1)S(1)}, bf16[256,128]{1,0:T(8,128)(2,1)S(1)}, u32[]{:S(2)}, u32[]{:S(2)}) collective-permute-start(bf16[256,128]{1,0:T(8,128)(2,1)S(1)} %get-tuple-element.4), channel_id=1, source_target_pairs={{0,16},{8,24},{16,0},{24,8},{1,17},{9,25},{17,1},{25,9},{2,18},{10... | collective-permute-start | bytes 196616 | tf_op jit(solution)/shard_map/ppermute | solution.py:120
  15.5 1.4 %collective-permute-start.9 = (bf16[256,128]{1,0:T(8,128)(2,1)S(1)}, bf16[256,128]{1,0:T(8,128)(2,1)S(1)}, u32[]{:S(2)}, u32[]{:S(2)}) collective-permute-start(bf16[256,128]{1,0:T(8,128)(2,1)S(1)} %get-tuple-element.3), channel_id=1, source_target_pairs={{0,24},{8,0},{16,8},{24,16},{1,25},{9,1},{17,9},{25,17},{2,26},{10... | collective-permute-start | bytes 196616 | tf_op jit(solution)/shard_map/ppermute | solution.py:120
  16.9 1.0 %constant_dynamic-update-slice_fusion.7 = bf16[8192,128]{1,0:T(8,128)(2,1)S(1)} fusion(bf16[1024,128]{1,0:T(8,128)(2,1)} %param.7), kind=kLoop, calls=%fused_computation.15 | loop fusion | bytes 524288
  17.9 0.3 collective-permute-done.7
  18.2 1.3 %collective-permute-start.2 = (bf16[1024,128]{1,0:T(8,128)(2,1)}, bf16[1024,128]{1,0:T(8,128)(2,1)S(1)}, u32[]{:S(2)}, u32[]{:S(2)}) collective-permute-start(bf16[1024,128]{1,0:T(8,128)(2,1)} %param.7), channel_id=1, source_target_pairs={{0,6},{1,7},{2,0},{3,1},{4,2},{5,3},{6,4},{7,5},{8,14},{9,15},{10,... | collective-permute-start | bytes 786440 | tf_op jit(solution)/shard_map/ppermute | solution.py:129
  19.6 0.0 collective-permute-done.8
  19.6 0.0 collective-permute-start.3
  19.6 0.2 collective-permute-done.9
  19.8 0.0 collective-permute-done
  19.8 0.4 collective-permute-start.4
  20.2 3.4 %collective-permute-done.1 = bf16[1024,128]{1,0:T(8,128)(2,1)S(1)} collective-permute-done((bf16[1024,128]{1,0:T(8,128)(2,1)}, bf16[1024,128]{1,0:T(8,128)(2,1)S(1)}, u32[]{:S(2)}, u32[]{:S(2)}) %collective-permute-start.1) | collective-permute-done | bytes 262176 | tf_op jit(solution)/shard_map/ppermute | solution.py:129
  23.6 0.0 collective-permute-start.5
  23.7 5.4 %collective-permute-done.2 = bf16[1024,128]{1,0:T(8,128)(2,1)S(1)} collective-permute-done((bf16[1024,128]{1,0:T(8,128)(2,1)}, bf16[1024,128]{1,0:T(8,128)(2,1)S(1)}, u32[]{:S(2)}, u32[]{:S(2)}) %collective-permute-start.2) | collective-permute-done | bytes 262176 | tf_op jit(solution)/shard_map/ppermute | solution.py:129
  29.1 0.0 collective-permute-start.6
  29.2 0.0 collective-permute-done.3
  29.2 0.0 collective-permute-done.4
  29.3 0.0 collective-permute-done.5
  29.3 1.3 %collective-permute-done.6 = bf16[1024,128]{1,0:T(8,128)(2,1)S(1)} collective-permute-done((bf16[1024,128]{1,0:T(8,128)(2,1)S(1)}, bf16[1024,128]{1,0:T(8,128)(2,1)S(1)}, u32[]{:S(2)}, u32[]{:S(2)}) %collective-permute-start.6) | collective-permute-done | bytes 262176 | tf_op jit(solution)/shard_map/ppermute | solution.py:131
  30.7 9.2 %shard_map.60 = bf16[768,128]{1,0:T(8,128)(2,1)S(1)} custom-call(bf16[768,128]{1,0:T(8,128)(2,1)S(1)} %pad_maximum_fusion.1.refs_0_, bf16[8192,128]{1,0:T(8,128)(2,1)S(1)} %constant_dynamic-update-slice_fusion.refs_1_), custom_call_target="tpu_custom_call" | custom-call | flops 3221225472 | bytes 2490368 | tf_op jit(solution)/shard_map/pallas_call | solution.py:92
  40.0 2.2 %collective-permute-start.10 = (bf16[256,128]{1,0:T(8,128)(2,1)S(1)}, bf16[256,128]{1,0:T(8,128)(2,1)S(1)}, u32[]{:S(2)}, u32[]{:S(2)}) collective-permute-start(bf16[256,128]{1,0:T(8,128)(2,1)S(1)} %get-tuple-element.6), channel_id=1, source_target_pairs={{0,24},{8,0},{16,8},{24,16},{1,25},{9,1},{17,9},{25,17},{2,26},{10... | collective-permute-start | bytes 196616 | tf_op jit(solution)/shard_map/ppermute | solution.py:120
  42.1 0.8 %collective-permute-start.11 = (bf16[256,128]{1,0:T(8,128)(2,1)S(1)}, bf16[256,128]{1,0:T(8,128)(2,1)S(1)}, u32[]{:S(2)}, u32[]{:S(2)}) collective-permute-start(bf16[256,128]{1,0:T(8,128)(2,1)S(1)} %get-tuple-element.8), channel_id=1, source_target_pairs={{0,16},{8,24},{16,0},{24,8},{1,17},{9,25},{17,1},{25,9},{2,18},{10... | collective-permute-start | bytes 196616 | tf_op jit(solution)/shard_map/ppermute | solution.py:120
  43.0 0.6 %collective-permute-start.12 = (bf16[256,128]{1,0:T(8,128)(2,1)S(1)}, bf16[256,128]{1,0:T(8,128)(2,1)S(1)}, u32[]{:S(2)}, u32[]{:S(2)}) collective-permute-start(bf16[256,128]{1,0:T(8,128)(2,1)S(1)} %get-tuple-element.7), channel_id=1, source_target_pairs={{0,8},{8,16},{16,24},{24,0},{1,9},{9,17},{17,25},{25,1},{2,10},{10... | collective-permute-start | bytes 196616 | tf_op jit(solution)/shard_map/ppermute | solution.py:120
  43.6 0.0 copy-start.1
  43.6 0.0 copy-start.2
  43.6 3.7 %shard_map.59 = bf16[256,128]{1,0:T(8,128)(2,1)S(1)} custom-call(bf16[256,128]{1,0:T(8,128)(2,1)S(1)} %get-tuple-element.2.refs_0_, bf16[8192,128]{1,0:T(8,128)(2,1)S(1)} %constant_dynamic-update-slice_fusion.refs_1_), custom_call_target="tpu_custom_call" | custom-call | flops 1073741824 | bytes 2228224 | tf_op jit(solution)/shard_map/pallas_call | solution.py:92
  47.3 0.0 collective-permute-done.10
  47.3 0.0 collective-permute-done.11
  47.3 0.8 %collective-permute-done.12 = bf16[256,128]{1,0:T(8,128)(2,1)S(1)} collective-permute-done((bf16[256,128]{1,0:T(8,128)(2,1)S(1)}, bf16[256,128]{1,0:T(8,128)(2,1)S(1)}, u32[]{:S(2)}, u32[]{:S(2)}) %collective-permute-start.12) | collective-permute-done | bytes 65568 | tf_op jit(solution)/shard_map/ppermute | solution.py:120
  48.2 1.3 %gather_fusion = bf16[512,128]{1,0:T(8,128)(2,1)S(1)} fusion(bf16[1024,128]{1,0:T(8,128)(2,1)S(1)} %pad_maximum_fusion, s32[1024]{0:T(1024)S(1)} %pad_clamp_fusion), kind=kCustom, calls=%fused_computation | custom fusion | bytes 264192 | tf_op jit(solution)/shard_map/gather | solution.py:152
  49.5 0.0 copy-done.1
  49.5 0.0 copy-done.2
  49.5 0.0 copy-start
  49.5 0.8 %subtract_convert_fusion = bf16[512,128]{1,0:T(8,128)(2,1)} fusion(bf16[512,128]{1,0:T(8,128)(2,1)S(1)} %gather_fusion, f32[512]{0:T(512)S(1)} %copy-done.2, bf16[512,128]{1,0:T(8,128)(2,1)S(1)} %copy-done.1), kind=kLoop, calls=%fused_computation.3 | loop fusion | flops 458752 | bytes 395264 | tf_op jit(solution)/shard_map/convert_element_type | solution.py:153
  50.3 0.0 copy-done
  (12 shorter events, 0.3 us)
Async XLA Ops:
  0.6 19.1 %collective-permute-start = (bf16[1024,128]{1,0:T(8,128)(2,1)}, bf16[1024,128]{1,0:T(8,128)(2,1)S(1)}, u32[]{:S(2)}, u32[]{:S(2)}) collective-permute-start(bf16[1024,128]{1,0:T(8,128)(2,1)} %param.7), channel_id=1, source_target_pairs={{0,2},{1,3},{2,4},{3,5},{4,6},{5,7},{6,0},{7,1},{8,10},{9,11},{10,... | collective-permute-start | bytes 786440 | tf_op jit(solution)/shard_map/ppermute | solution.py:129
  3.7 19.9 %collective-permute-start.1 = (bf16[1024,128]{1,0:T(8,128)(2,1)}, bf16[1024,128]{1,0:T(8,128)(2,1)S(1)}, u32[]{:S(2)}, u32[]{:S(2)}) collective-permute-start(bf16[1024,128]{1,0:T(8,128)(2,1)} %param.7), channel_id=1, source_target_pairs={{0,4},{1,5},{2,6},{3,7},{4,0},{5,1},{6,2},{7,3},{8,12},{9,13},{10,... | collective-permute-start | bytes 786440 | tf_op jit(solution)/shard_map/ppermute | solution.py:129
  12.4 5.8 %collective-permute-start.7 = (bf16[256,128]{1,0:T(8,128)(2,1)S(1)}, bf16[256,128]{1,0:T(8,128)(2,1)S(1)}, u32[]{:S(2)}, u32[]{:S(2)}) collective-permute-start(bf16[256,128]{1,0:T(8,128)(2,1)S(1)} %get-tuple-element.5), channel_id=1, source_target_pairs={{0,8},{8,16},{16,24},{24,0},{1,9},{9,17},{17,25},{25,1},{2,10},{10... | collective-permute-start | bytes 196616 | tf_op jit(solution)/shard_map/ppermute | solution.py:120
  14.0 5.6 %collective-permute-start.8 = (bf16[256,128]{1,0:T(8,128)(2,1)S(1)}, bf16[256,128]{1,0:T(8,128)(2,1)S(1)}, u32[]{:S(2)}, u32[]{:S(2)}) collective-permute-start(bf16[256,128]{1,0:T(8,128)(2,1)S(1)} %get-tuple-element.4), channel_id=1, source_target_pairs={{0,16},{8,24},{16,0},{24,8},{1,17},{9,25},{17,1},{25,9},{2,18},{10... | collective-permute-start | bytes 196616 | tf_op jit(solution)/shard_map/ppermute | solution.py:120
  15.5 4.3 %collective-permute-start.9 = (bf16[256,128]{1,0:T(8,128)(2,1)S(1)}, bf16[256,128]{1,0:T(8,128)(2,1)S(1)}, u32[]{:S(2)}, u32[]{:S(2)}) collective-permute-start(bf16[256,128]{1,0:T(8,128)(2,1)S(1)} %get-tuple-element.3), channel_id=1, source_target_pairs={{0,24},{8,0},{16,8},{24,16},{1,25},{9,1},{17,9},{25,17},{2,26},{10... | collective-permute-start | bytes 196616 | tf_op jit(solution)/shard_map/ppermute | solution.py:120
  18.2 10.9 %collective-permute-start.2 = (bf16[1024,128]{1,0:T(8,128)(2,1)}, bf16[1024,128]{1,0:T(8,128)(2,1)S(1)}, u32[]{:S(2)}, u32[]{:S(2)}) collective-permute-start(bf16[1024,128]{1,0:T(8,128)(2,1)} %param.7), channel_id=1, source_target_pairs={{0,6},{1,7},{2,0},{3,1},{4,2},{5,3},{6,4},{7,5},{8,14},{9,15},{10,... | collective-permute-start | bytes 786440 | tf_op jit(solution)/shard_map/ppermute | solution.py:129
  19.6 9.6 %collective-permute-start.3 = (bf16[1024,128]{1,0:T(8,128)(2,1)}, bf16[1024,128]{1,0:T(8,128)(2,1)S(1)}, u32[]{:S(2)}, u32[]{:S(2)}) collective-permute-start(bf16[1024,128]{1,0:T(8,128)(2,1)} %param.7), channel_id=1, source_target_pairs={{0,1},{1,0},{2,3},{3,2},{4,5},{5,4},{6,7},{7,6},{8,9},{9,8},{10,11... | collective-permute-start | bytes 786440 | tf_op jit(solution)/shard_map/ppermute | solution.py:131
  19.8 9.5 %collective-permute-start.4 = (bf16[1024,128]{1,0:T(8,128)(2,1)S(1)}, bf16[1024,128]{1,0:T(8,128)(2,1)S(1)}, u32[]{:S(2)}, u32[]{:S(2)}) collective-permute-start(bf16[1024,128]{1,0:T(8,128)(2,1)S(1)} %collective-permute-done), channel_id=1, source_target_pairs={{0,1},{1,0},{2,3},{3,2},{4,5},{5,4},{6,7},{7,6},{8,9},{9,8},{10,11... | collective-permute-start | bytes 786440 | tf_op jit(solution)/shard_map/ppermute | solution.py:131
  23.6 5.6 %collective-permute-start.5 = (bf16[1024,128]{1,0:T(8,128)(2,1)S(1)}, bf16[1024,128]{1,0:T(8,128)(2,1)S(1)}, u32[]{:S(2)}, u32[]{:S(2)}) collective-permute-start(bf16[1024,128]{1,0:T(8,128)(2,1)S(1)} %collective-permute-done.1), channel_id=1, source_target_pairs={{0,1},{1,0},{2,3},{3,2},{4,5},{5,4},{6,7},{7,6},{8,9},{9,8},{10,11... | collective-permute-start | bytes 786440 | tf_op jit(solution)/shard_map/ppermute | solution.py:131
  29.1 1.5 %collective-permute-start.6 = (bf16[1024,128]{1,0:T(8,128)(2,1)S(1)}, bf16[1024,128]{1,0:T(8,128)(2,1)S(1)}, u32[]{:S(2)}, u32[]{:S(2)}) collective-permute-start(bf16[1024,128]{1,0:T(8,128)(2,1)S(1)} %collective-permute-done.2), channel_id=1, source_target_pairs={{0,1},{1,0},{2,3},{3,2},{4,5},{5,4},{6,7},{7,6},{8,9},{9,8},{10,11... | collective-permute-start | bytes 786440 | tf_op jit(solution)/shard_map/ppermute | solution.py:131
  40.0 7.3 %collective-permute-start.10 = (bf16[256,128]{1,0:T(8,128)(2,1)S(1)}, bf16[256,128]{1,0:T(8,128)(2,1)S(1)}, u32[]{:S(2)}, u32[]{:S(2)}) collective-permute-start(bf16[256,128]{1,0:T(8,128)(2,1)S(1)} %get-tuple-element.6), channel_id=1, source_target_pairs={{0,24},{8,0},{16,8},{24,16},{1,25},{9,1},{17,9},{25,17},{2,26},{10... | collective-permute-start | bytes 196616 | tf_op jit(solution)/shard_map/ppermute | solution.py:120
  42.1 5.2 %collective-permute-start.11 = (bf16[256,128]{1,0:T(8,128)(2,1)S(1)}, bf16[256,128]{1,0:T(8,128)(2,1)S(1)}, u32[]{:S(2)}, u32[]{:S(2)}) collective-permute-start(bf16[256,128]{1,0:T(8,128)(2,1)S(1)} %get-tuple-element.8), channel_id=1, source_target_pairs={{0,16},{8,24},{16,0},{24,8},{1,17},{9,25},{17,1},{25,9},{2,18},{10... | collective-permute-start | bytes 196616 | tf_op jit(solution)/shard_map/ppermute | solution.py:120
  43.0 5.2 %collective-permute-start.12 = (bf16[256,128]{1,0:T(8,128)(2,1)S(1)}, bf16[256,128]{1,0:T(8,128)(2,1)S(1)}, u32[]{:S(2)}, u32[]{:S(2)}) collective-permute-start(bf16[256,128]{1,0:T(8,128)(2,1)S(1)} %get-tuple-element.7), channel_id=1, source_target_pairs={{0,8},{8,16},{16,24},{24,0},{1,9},{9,17},{17,25},{25,1},{2,10},{10... | collective-permute-start | bytes 196616 | tf_op jit(solution)/shard_map/ppermute | solution.py:120
  43.6 5.9 %copy-start.1 = (bf16[512,128]{1,0:T(8,128)(2,1)S(1)}, bf16[512,128]{1,0:T(8,128)(2,1)}, u32[]{:S(2)}) copy-start(bf16[512,128]{1,0:T(8,128)(2,1)} %param.4) | copy-start | bytes 393220
  43.6 6.0 %copy-start.2 = (f32[512]{0:T(512)S(1)}, f32[512]{0:T(512)}, u32[]{:S(2)}) copy-start(f32[512]{0:T(512)} %param.5) | copy-start | bytes 6148
  49.5 0.8 %copy-start = (bf16[512,128]{1,0:T(8,128)(2,1)}, bf16[512,128]{1,0:T(8,128)(2,1)S(1)}, u32[]{:S(2)}) copy-start(bf16[512,128]{1,0:T(8,128)(2,1)S(1)} %gather_fusion) | copy-start | bytes 393220
where the time goes:
time: 50.6 us; the launch traced here: 50.3 us
  starting transfers between devices  15.6 us (31%)
  Pallas kernels  12.9 us (25%)
  waiting for transfers between devices  11.5 us (23%)
  other arithmetic  6.67 us (13%)
  local copies, waits for them, and re-layouts  2.82 us (6%)
  between operations  0.82 us (2%)
    pallas_call x2, Pallas kernels, soft_part(): pl.pallas_call(functools.partial(_soft_kernel, chunk=chunk, beta=1.0 / ma...  12.9 us
    ppermute x3, waiting for transfers between devices, _gather_partition(): pieces.append(lax.ppermute(centroids, 'blk', pairs))  8.85 us
    ppermute x6, starting transfers between devices, _shift(): return lax.ppermute(x, axis, [(i, (i + d) % n) for i in range(n)])  8.09 us
    ppermute x3, starting transfers between devices, _gather_partition(): pieces.append(lax.ppermute(centroids, 'blk', pairs))  7.04 us
    scatter x1, other arithmetic, _local(): jnp.zeros((loops * cap, width), jnp.bfloat16).at[slots].set(dequant)  2.28 us
    another operation x2, other arithmetic  1.39 us
    gather x1, local copies, waits for them, and re-layouts, _local(): mine = jnp.concatenate([ret[d] for d in range(loops)], axis=0)[slots]  1.34 us
    ppermute x6, waiting for transfers between devices, _shift(): return lax.ppermute(x, axis, [(i, (i + d) % n) for i in range(n)])  1.34 us
  transfers between devices with their start and end apart: 13, of which 6 were waited for; matrix products, arithmetic and copies ran while one was open for 14% of the time, Pallas kernels for 7%

commit v1 on v0

--- a/solution.py
+++ b/solution.py
@@ -149,7 +149,12 @@
     first = soft_part(jnp.concatenate(arrived[1:], axis=0), part, final=True)
     ret = {d: _shift(first[(d - 1) * cap:d * cap], "cell", loops, -d) for d in range(1, loops)}
     ret[0] = soft_part(arrived[0], part, final=True)
-    mine = jnp.concatenate([ret[d] for d in range(loops)], axis=0)[slots]
+    rel = slots // cap
+    own = ret[0][slots % cap]
+    remote = jnp.concatenate([ret[d] for d in range(1, loops)], axis=0)
+    pick = (slots[:, None] - cap == jnp.arange(remote.shape[0], dtype=jnp.int32)[None, :])
+    tail = jnp.dot(pick.astype(jnp.bfloat16), remote, preferred_element_type=jnp.float32)
+    mine = jnp.where((rel == 0)[:, None], own, tail.astype(jnp.bfloat16))
     residual = (dequant.astype(jnp.float32) - mine.astype(jnp.float32)).astype(jnp.bfloat16)
     return (mine, residual)
 

time: 50.6 us -> 50.3 us (level)
  waiting for transfers between devices: 11.5 us -> 10.7 us
    ppermute x6, waiting for transfers between devices: 1.34 us -> 0.5 us  [_shift(): return lax.ppermute(x, axis, [(i, (i + d) % n) for i in range(n)])]
    eq x0 -> x1, other arithmetic: none -> 0.71 us  [_local(): mine = jnp.where((rel == 0)[:, None], own, tail.astype(jnp.bfloat16))]
    select_n x1 -> x0, other arithmetic: 0.7 us -> none  [_local(): jnp.zeros((loops * cap, width), jnp.bfloat16).at[slots].set(dequant)]
    unnamed x13 -> x11, local copies, waits for them, and re-layouts: 1.19 us -> 1.19 us
  transfers between devices with their start and end apart: 13 -> 13, of which waited for: 6 -> 5; matrix products, arithmetic and copies ran while one was open for 14% -> 17% of each run, Pallas kernels for 7% -> 7%
where the time goes in v1:
time: 50.3 us; the launch traced here: 50 us
  starting transfers between devices  15.6 us (31%)
  Pallas kernels  12.9 us (26%)
  waiting for transfers between devices  10.7 us (21%)
  other arithmetic  6.78 us (13%)
  local copies, waits for them, and re-layouts  2.82 us (6%)
  between operations  0.84 us (2%)
    pallas_call x2, Pallas kernels, soft_part(): pl.pallas_call(functools.partial(_soft_kernel, chunk=chunk, beta=1.0 / ma...  12.9 us
    ppermute x3, waiting for transfers between devices, _gather_partition(): pieces.append(lax.ppermute(centroids, 'blk', pairs))  8.83 us
    ppermute x6, starting transfers between devices, _shift(): return lax.ppermute(x, axis, [(i, (i + d) % n) for i in range(n)])  8.09 us
    ppermute x3, starting transfers between devices, _gather_partition(): pieces.append(lax.ppermute(centroids, 'blk', pairs))  7.04 us
    scatter x1, other arithmetic, _local(): jnp.zeros((loops * cap, width), jnp.bfloat16).at[slots].set(dequant)  2.29 us
    another operation x2, other arithmetic  1.39 us
    gather x1, local copies, waits for them, and re-layouts, _local(): own = ret[0][slots % cap]  1.34 us
    ppermute x4, waiting for transfers between devices, _gather_partition(): swapped = [lax.ppermute(p, 'blk', swap) for p in pieces]  1.32 us
  transfers between devices with their start and end apart: 13, of which 5 were waited for; matrix products, arithmetic and copies ran while one was open for 17% of the time, Pallas kernels for 7%

profile of v1, /device:TPU:0, one launch (start us, length us, event | category | flops | bytes accessed | tf_op | source)
XLA Modules:
  0.0 50.0 jit_solution(9875028213013177121)
XLA Ops:
  0.6 3.1 %collective-permute-start = (bf16[1024,128]{1,0:T(8,128)(2,1)}, bf16[1024,128]{1,0:T(8,128)(2,1)S(1)}, u32[]{:S(2)}, u32[]{:S(2)}) collective-permute-start(bf16[1024,128]{1,0:T(8,128)(2,1)} %param.7), channel_id=1, source_target_pairs={{0,2},{1,3},{2,4},{3,5},{4,6},{5,7},{6,0},{7,1},{8,10},{9,11},{10,... | collective-permute-start | bytes 786440 | tf_op jit(solution)/shard_map/ppermute | solution.py:129
  3.7 2.6 %collective-permute-start.1 = (bf16[1024,128]{1,0:T(8,128)(2,1)}, bf16[1024,128]{1,0:T(8,128)(2,1)S(1)}, u32[]{:S(2)}, u32[]{:S(2)}) collective-permute-start(bf16[1024,128]{1,0:T(8,128)(2,1)} %param.7), channel_id=1, source_target_pairs={{0,4},{1,5},{2,6},{3,7},{4,0},{5,1},{6,2},{7,3},{8,12},{9,13},{10,... | collective-permute-start | bytes 786440 | tf_op jit(solution)/shard_map/ppermute | solution.py:129
  6.3 0.7 %fusion.12 = s32[4,4,128]{2,1,0:T(4,128)S(1)} fusion(s32[4,128]{1,0:T(4,128)} %bitcast.16), kind=kLoop, calls=%fused_computation.32 | loop fusion | flops 4096 | bytes 10240 | tf_op jit(solution)/shard_map/convert_element_type | solution.py:142
  7.0 1.2 %reduce-window.6 = s32[4,4,128]{2,1,0:T(4,128)S(1)} reduce-window(s32[4,4,128]{2,1,0:T(4,128)S(1)} %fusion.12, s32[]{:T(128)} %constant.49.clone.1), window={size=1x1x128 pad=0_0x0_0x127_0}, to_apply=%region_0.0 | reduce-window | flops 260096 | bytes 16388 | tf_op jit(solution)/shard_map/reduce-window
  8.2 0.2 slice_reduce_fusion
  8.4 0.2 reduce-window.9
  8.6 0.1 add_bitcast_fusion
  8.7 0.7 %fusion.11 = s32[512]{0:T(512)S(1)} fusion(s32[1,4,4,128]{3,2,1,0:T(4,128)S(1)} %add_bitcast_fusion, s32[512]{0:T(512)} %param.6), kind=kLoop, calls=%fused_computation.27 | loop fusion | flops 5632 | bytes 12288 | tf_op jit(solution)/shard_map/reduce_sum | solution.py:143
  9.4 0.7 %fusion.16 = (pred[512]{0:T(512)(128)(4,1)S(1)}, s32[512]{0:T(512)S(1)}) fusion(s32[512]{0:T(512)S(1)} %fusion.11, s32[512]{0:T(512)} %param.6, s32[]{:T(128)S(6)} %axis_index.15), kind=kLoop, calls=%fused_computation.47 | loop fusion | flops 15872 | bytes 6660 | tf_op jit(solution)/shard_map/eq | solution.py:157
  10.1 2.3 %scatter_custom_fusion = bf16[1024,128]{1,0:T(8,128)(2,1)S(1)} fusion(s32[512]{0:T(512)S(1)} %get-tuple-element.14, bf16[]{:T(256)} %constant.57.clone.1, bf16[512,128]{1,0:T(8,128)(2,1)} %param.4, f32[512]{0:T(512)} %param.5), kind=kCustom, calls=%fused_computation.14 | custom fusion | flops 196608 | bytes 395266 | tf_op jit(solution)/shard_map/scatter | solution.py:145
  12.4 1.5 %collective-permute-start.7 = (bf16[256,128]{1,0:T(8,128)(2,1)S(1)}, bf16[256,128]{1,0:T(8,128)(2,1)S(1)}, u32[]{:S(2)}, u32[]{:S(2)}) collective-permute-start(bf16[256,128]{1,0:T(8,128)(2,1)S(1)} %get-tuple-element.6), channel_id=1, source_target_pairs={{0,8},{8,16},{16,24},{24,0},{1,9},{9,17},{17,25},{25,1},{2,10},{10... | collective-permute-start | bytes 196616 | tf_op jit(solution)/shard_map/ppermute | solution.py:120
  14.0 1.5 %collective-permute-start.8 = (bf16[256,128]{1,0:T(8,128)(2,1)S(1)}, bf16[256,128]{1,0:T(8,128)(2,1)S(1)}, u32[]{:S(2)}, u32[]{:S(2)}) collective-permute-start(bf16[256,128]{1,0:T(8,128)(2,1)S(1)} %get-tuple-element.8), channel_id=1, source_target_pairs={{0,16},{8,24},{16,0},{24,8},{1,17},{9,25},{17,1},{25,9},{2,18},{10... | collective-permute-start | bytes 196616 | tf_op jit(solution)/shard_map/ppermute | solution.py:120
  15.5 1.4 %collective-permute-start.9 = (bf16[256,128]{1,0:T(8,128)(2,1)S(1)}, bf16[256,128]{1,0:T(8,128)(2,1)S(1)}, u32[]{:S(2)}, u32[]{:S(2)}) collective-permute-start(bf16[256,128]{1,0:T(8,128)(2,1)S(1)} %get-tuple-element.7), channel_id=1, source_target_pairs={{0,24},{8,0},{16,8},{24,16},{1,25},{9,1},{17,9},{25,17},{2,26},{10... | collective-permute-start | bytes 196616 | tf_op jit(solution)/shard_map/ppermute | solution.py:120
  16.9 1.0 %constant_dynamic-update-slice_fusion.7 = bf16[8192,128]{1,0:T(8,128)(2,1)S(1)} fusion(bf16[1024,128]{1,0:T(8,128)(2,1)} %param.7), kind=kLoop, calls=%fused_computation.24 | loop fusion | bytes 524288
  17.9 0.3 collective-permute-done.7
  18.3 1.3 %collective-permute-start.2 = (bf16[1024,128]{1,0:T(8,128)(2,1)}, bf16[1024,128]{1,0:T(8,128)(2,1)S(1)}, u32[]{:S(2)}, u32[]{:S(2)}) collective-permute-start(bf16[1024,128]{1,0:T(8,128)(2,1)} %param.7), channel_id=1, source_target_pairs={{0,6},{1,7},{2,0},{3,1},{4,2},{5,3},{6,4},{7,5},{8,14},{9,15},{10,... | collective-permute-start | bytes 786440 | tf_op jit(solution)/shard_map/ppermute | solution.py:129
  19.6 0.0 collective-permute-done.8
  19.6 0.0 collective-permute-start.3
  19.6 0.2 collective-permute-done.9
  19.8 0.0 collective-permute-done
  19.8 0.4 collective-permute-start.4
  20.3 3.4 %collective-permute-done.1 = bf16[1024,128]{1,0:T(8,128)(2,1)S(1)} collective-permute-done((bf16[1024,128]{1,0:T(8,128)(2,1)}, bf16[1024,128]{1,0:T(8,128)(2,1)S(1)}, u32[]{:S(2)}, u32[]{:S(2)}) %collective-permute-start.1) | collective-permute-done | bytes 262176 | tf_op jit(solution)/shard_map/ppermute | solution.py:129
  23.6 0.0 collective-permute-start.5
  23.7 5.4 %collective-permute-done.2 = bf16[1024,128]{1,0:T(8,128)(2,1)S(1)} collective-permute-done((bf16[1024,128]{1,0:T(8,128)(2,1)}, bf16[1024,128]{1,0:T(8,128)(2,1)S(1)}, u32[]{:S(2)}, u32[]{:S(2)}) %collective-permute-start.2) | collective-permute-done | bytes 262176 | tf_op jit(solution)/shard_map/ppermute | solution.py:129
  29.1 0.0 collective-permute-start.6
  29.2 0.0 collective-permute-done.3
  29.2 0.0 collective-permute-done.4
  29.3 0.0 collective-permute-done.5
  29.3 1.3 %collective-permute-done.6 = bf16[1024,128]{1,0:T(8,128)(2,1)S(1)} collective-permute-done((bf16[1024,128]{1,0:T(8,128)(2,1)S(1)}, bf16[1024,128]{1,0:T(8,128)(2,1)S(1)}, u32[]{:S(2)}, u32[]{:S(2)}) %collective-permute-start.6) | collective-permute-done | bytes 262176 | tf_op jit(solution)/shard_map/ppermute | solution.py:131
  30.7 9.2 %shard_map.60 = bf16[768,128]{1,0:T(8,128)(2,1)S(1)} custom-call(bf16[768,128]{1,0:T(8,128)(2,1)S(1)} %pad_maximum_fusion.refs_0_, bf16[8192,128]{1,0:T(8,128)(2,1)S(1)} %constant_dynamic-update-slice_fusion.refs_1_), custom_call_target="tpu_custom_call" | custom-call | flops 3221225472 | bytes 2490368 | tf_op jit(solution)/shard_map/pallas_call | solution.py:92
  40.0 2.2 %collective-permute-start.10 = (bf16[256,128]{1,0:T(8,128)(2,1)S(1)}, bf16[256,128]{1,0:T(8,128)(2,1)S(1)}, u32[]{:S(2)}, u32[]{:S(2)}) collective-permute-start(bf16[256,128]{1,0:T(8,128)(2,1)S(1)} %get-tuple-element.10), channel_id=1, source_target_pairs={{0,24},{8,0},{16,8},{24,16},{1,25},{9,1},{17,9},{25,17},{2,26},{10... | collective-permute-start | bytes 196616 | tf_op jit(solution)/shard_map/ppermute | solution.py:120
  42.2 0.8 %collective-permute-start.11 = (bf16[256,128]{1,0:T(8,128)(2,1)S(1)}, bf16[256,128]{1,0:T(8,128)(2,1)S(1)}, u32[]{:S(2)}, u32[]{:S(2)}) collective-permute-start(bf16[256,128]{1,0:T(8,128)(2,1)S(1)} %get-tuple-element.12), channel_id=1, source_target_pairs={{0,16},{8,24},{16,0},{24,8},{1,17},{9,25},{17,1},{25,9},{2,18},{10... | collective-permute-start | bytes 196616 | tf_op jit(solution)/shard_map/ppermute | solution.py:120
  43.0 0.6 %collective-permute-start.12 = (bf16[256,128]{1,0:T(8,128)(2,1)S(1)}, bf16[256,128]{1,0:T(8,128)(2,1)S(1)}, u32[]{:S(2)}, u32[]{:S(2)}) collective-permute-start(bf16[256,128]{1,0:T(8,128)(2,1)S(1)} %get-tuple-element.11), channel_id=1, source_target_pairs={{0,8},{8,16},{16,24},{24,0},{1,9},{9,17},{17,25},{25,1},{2,10},{10... | collective-permute-start | bytes 196616 | tf_op jit(solution)/shard_map/ppermute | solution.py:120
  43.6 3.7 %shard_map.59 = bf16[256,128]{1,0:T(8,128)(2,1)S(1)} custom-call(bf16[256,128]{1,0:T(8,128)(2,1)S(1)} %get-tuple-element.9.refs_0_, bf16[8192,128]{1,0:T(8,128)(2,1)S(1)} %constant_dynamic-update-slice_fusion.refs_1_), custom_call_target="tpu_custom_call" | custom-call | flops 1073741824 | bytes 2228224 | tf_op jit(solution)/shard_map/pallas_call | solution.py:92
  47.3 0.0 copy-start
  47.3 0.0 copy-start.1
  47.3 1.3 %gather_fusion = bf16[512,128]{1,0:T(8,128)(2,1)S(1)} fusion(bf16[256,128]{1,0:T(8,128)(2,1)S(1)} %shard_map.59, s32[1024]{0:T(1024)S(1)} %pad_clamp_fusion), kind=kCustom, calls=%fused_computation | custom fusion | bytes 264192 | tf_op jit(solution)/shard_map/gather | solution.py:153
  48.6 0.0 collective-permute-done.10
  48.7 0.0 collective-permute-done.11
  48.7 0.0 collective-permute-done.12
  48.7 0.4 fusion.1
  49.1 0.0 copy-done
  49.1 0.0 copy-done.1
  49.1 0.9 %subtract_convert_fusion = (bf16[512,128]{1,0:T(8,128)(2,1)}, bf16[512,128]{1,0:T(8,128)(2,1)}) fusion(f32[512]{0:T(512)S(1)} %copy-done.1, bf16[512,128]{1,0:T(8,128)(2,1)S(1)} %copy-done, bf16[512,128]{1,0:T(8,128)(2,1)S(1)} %gather_fusion, bf16[512,128]{1,0:T(8,128)(2,1)S(1)} %fusion.1, pred[512]{0:T(512)(128)(4,1)S(1)} %get-tuple-element.4), kind=kLoop, calls=%fused_computation.6 | loop fusion | flops 524288 | bytes 657920 | tf_op jit(solution)/shard_map/convert_element_type | solution.py:158
  (12 shorter events, 0.3 us)
Async XLA Ops:
  0.6 19.2 %collective-permute-start = (bf16[1024,128]{1,0:T(8,128)(2,1)}, bf16[1024,128]{1,0:T(8,128)(2,1)S(1)}, u32[]{:S(2)}, u32[]{:S(2)}) collective-permute-start(bf16[1024,128]{1,0:T(8,128)(2,1)} %param.7), channel_id=1, source_target_pairs={{0,2},{1,3},{2,4},{3,5},{4,6},{5,7},{6,0},{7,1},{8,10},{9,11},{10,... | collective-permute-start | bytes 786440 | tf_op jit(solution)/shard_map/ppermute | solution.py:129
  3.7 19.9 %collective-permute-start.1 = (bf16[1024,128]{1,0:T(8,128)(2,1)}, bf16[1024,128]{1,0:T(8,128)(2,1)S(1)}, u32[]{:S(2)}, u32[]{:S(2)}) collective-permute-start(bf16[1024,128]{1,0:T(8,128)(2,1)} %param.7), channel_id=1, source_target_pairs={{0,4},{1,5},{2,6},{3,7},{4,0},{5,1},{6,2},{7,3},{8,12},{9,13},{10,... | collective-permute-start | bytes 786440 | tf_op jit(solution)/shard_map/ppermute | solution.py:129
  12.4 5.8 %collective-permute-start.7 = (bf16[256,128]{1,0:T(8,128)(2,1)S(1)}, bf16[256,128]{1,0:T(8,128)(2,1)S(1)}, u32[]{:S(2)}, u32[]{:S(2)}) collective-permute-start(bf16[256,128]{1,0:T(8,128)(2,1)S(1)} %get-tuple-element.6), channel_id=1, source_target_pairs={{0,8},{8,16},{16,24},{24,0},{1,9},{9,17},{17,25},{25,1},{2,10},{10... | collective-permute-start | bytes 196616 | tf_op jit(solution)/shard_map/ppermute | solution.py:120
  14.0 5.6 %collective-permute-start.8 = (bf16[256,128]{1,0:T(8,128)(2,1)S(1)}, bf16[256,128]{1,0:T(8,128)(2,1)S(1)}, u32[]{:S(2)}, u32[]{:S(2)}) collective-permute-start(bf16[256,128]{1,0:T(8,128)(2,1)S(1)} %get-tuple-element.8), channel_id=1, source_target_pairs={{0,16},{8,24},{16,0},{24,8},{1,17},{9,25},{17,1},{25,9},{2,18},{10... | collective-permute-start | bytes 196616 | tf_op jit(solution)/shard_map/ppermute | solution.py:120
  15.5 4.3 %collective-permute-start.9 = (bf16[256,128]{1,0:T(8,128)(2,1)S(1)}, bf16[256,128]{1,0:T(8,128)(2,1)S(1)}, u32[]{:S(2)}, u32[]{:S(2)}) collective-permute-start(bf16[256,128]{1,0:T(8,128)(2,1)S(1)} %get-tuple-element.7), channel_id=1, source_target_pairs={{0,24},{8,0},{16,8},{24,16},{1,25},{9,1},{17,9},{25,17},{2,26},{10... | collective-permute-start | bytes 196616 | tf_op jit(solution)/shard_map/ppermute | solution.py:120
  18.3 10.9 %collective-permute-start.2 = (bf16[1024,128]{1,0:T(8,128)(2,1)}, bf16[1024,128]{1,0:T(8,128)(2,1)S(1)}, u32[]{:S(2)}, u32[]{:S(2)}) collective-permute-start(bf16[1024,128]{1,0:T(8,128)(2,1)} %param.7), channel_id=1, source_target_pairs={{0,6},{1,7},{2,0},{3,1},{4,2},{5,3},{6,4},{7,5},{8,14},{9,15},{10,... | collective-permute-start | bytes 786440 | tf_op jit(solution)/shard_map/ppermute | solution.py:129
  19.6 9.6 %collective-permute-start.3 = (bf16[1024,128]{1,0:T(8,128)(2,1)}, bf16[1024,128]{1,0:T(8,128)(2,1)S(1)}, u32[]{:S(2)}, u32[]{:S(2)}) collective-permute-start(bf16[1024,128]{1,0:T(8,128)(2,1)} %param.7), channel_id=1, source_target_pairs={{0,1},{1,0},{2,3},{3,2},{4,5},{5,4},{6,7},{7,6},{8,9},{9,8},{10,11... | collective-permute-start | bytes 786440 | tf_op jit(solution)/shard_map/ppermute | solution.py:131
  19.8 9.4 %collective-permute-start.4 = (bf16[1024,128]{1,0:T(8,128)(2,1)S(1)}, bf16[1024,128]{1,0:T(8,128)(2,1)S(1)}, u32[]{:S(2)}, u32[]{:S(2)}) collective-permute-start(bf16[1024,128]{1,0:T(8,128)(2,1)S(1)} %collective-permute-done), channel_id=1, source_target_pairs={{0,1},{1,0},{2,3},{3,2},{4,5},{5,4},{6,7},{7,6},{8,9},{9,8},{10,11... | collective-permute-start | bytes 786440 | tf_op jit(solution)/shard_map/ppermute | solution.py:131
  23.6 5.6 %collective-permute-start.5 = (bf16[1024,128]{1,0:T(8,128)(2,1)S(1)}, bf16[1024,128]{1,0:T(8,128)(2,1)S(1)}, u32[]{:S(2)}, u32[]{:S(2)}) collective-permute-start(bf16[1024,128]{1,0:T(8,128)(2,1)S(1)} %collective-permute-done.1), channel_id=1, source_target_pairs={{0,1},{1,0},{2,3},{3,2},{4,5},{5,4},{6,7},{7,6},{8,9},{9,8},{10,11... | collective-permute-start | bytes 786440 | tf_op jit(solution)/shard_map/ppermute | solution.py:131
  29.1 1.5 %collective-permute-start.6 = (bf16[1024,128]{1,0:T(8,128)(2,1)S(1)}, bf16[1024,128]{1,0:T(8,128)(2,1)S(1)}, u32[]{:S(2)}, u32[]{:S(2)}) collective-permute-start(bf16[1024,128]{1,0:T(8,128)(2,1)S(1)} %collective-permute-done.2), channel_id=1, source_target_pairs={{0,1},{1,0},{2,3},{3,2},{4,5},{5,4},{6,7},{7,6},{8,9},{9,8},{10,11... | collective-permute-start | bytes 786440 | tf_op jit(solution)/shard_map/ppermute | solution.py:131
  40.0 8.7 %collective-permute-start.10 = (bf16[256,128]{1,0:T(8,128)(2,1)S(1)}, bf16[256,128]{1,0:T(8,128)(2,1)S(1)}, u32[]{:S(2)}, u32[]{:S(2)}) collective-permute-start(bf16[256,128]{1,0:T(8,128)(2,1)S(1)} %get-tuple-element.10), channel_id=1, source_target_pairs={{0,24},{8,0},{16,8},{24,16},{1,25},{9,1},{17,9},{25,17},{2,26},{10... | collective-permute-start | bytes 196616 | tf_op jit(solution)/shard_map/ppermute | solution.py:120
  42.2 6.5 %collective-permute-start.11 = (bf16[256,128]{1,0:T(8,128)(2,1)S(1)}, bf16[256,128]{1,0:T(8,128)(2,1)S(1)}, u32[]{:S(2)}, u32[]{:S(2)}) collective-permute-start(bf16[256,128]{1,0:T(8,128)(2,1)S(1)} %get-tuple-element.12), channel_id=1, source_target_pairs={{0,16},{8,24},{16,0},{24,8},{1,17},{9,25},{17,1},{25,9},{2,18},{10... | collective-permute-start | bytes 196616 | tf_op jit(solution)/shard_map/ppermute | solution.py:120
  43.0 5.7 %collective-permute-start.12 = (bf16[256,128]{1,0:T(8,128)(2,1)S(1)}, bf16[256,128]{1,0:T(8,128)(2,1)S(1)}, u32[]{:S(2)}, u32[]{:S(2)}) collective-permute-start(bf16[256,128]{1,0:T(8,128)(2,1)S(1)} %get-tuple-element.11), channel_id=1, source_target_pairs={{0,8},{8,16},{16,24},{24,0},{1,9},{9,17},{17,25},{25,1},{2,10},{10... | collective-permute-start | bytes 196616 | tf_op jit(solution)/shard_map/ppermute | solution.py:120
  47.3 1.8 %copy-start = (bf16[512,128]{1,0:T(8,128)(2,1)S(1)}, bf16[512,128]{1,0:T(8,128)(2,1)}, u32[]{:S(2)}) copy-start(bf16[512,128]{1,0:T(8,128)(2,1)} %param.4) | copy-start | bytes 393220
  47.3 1.8 %copy-start.1 = (f32[512]{0:T(512)S(1)}, f32[512]{0:T(512)}, u32[]{:S(2)}) copy-start(f32[512]{0:T(512)} %param.5) | copy-start | bytes 6148

commit v2 on v0

--- a/solution.py
+++ b/solution.py
@@ -123,10 +123,27 @@
 def _gather_partition(centroids):
     n_blk = lax.axis_size("blk")
     n_chip = n_blk // 2
-    pieces = [centroids]
-    for d in range(1, n_chip):
-        pairs = [(k * 2 + c, ((k + d) % n_chip) * 2 + c) for k in range(n_chip) for c in range(2)]
-        pieces.append(lax.ppermute(centroids, "blk", pairs))
+    chip = lax.axis_index("blk") // 2
+
+    def over_chips(x, moves):
+        return lax.ppermute(x, "blk", [(k * 2 + c, j * 2 + c) for k, j in moves for c in range(2)])
+
+    if n_chip == 4:
+        up1 = over_chips(centroids, [(0, 1), (1, 2), (2, 3)])
+        dn1 = over_chips(centroids, [(1, 0), (2, 1), (3, 2)])
+        up2 = over_chips(up1, [(1, 2), (2, 3)])
+        dn2 = over_chips(dn1, [(2, 1), (1, 0)])
+        up3 = over_chips(up2, [(2, 3)])
+        dn3 = over_chips(dn2, [(1, 0)])
+        near = jnp.where(chip == 0, dn1, up1)
+        mid = jnp.where(chip == 0, dn2, jnp.where(chip == 1, dn1, up2))
+        far = jnp.where(chip == 0, dn3, jnp.where(chip == 1, dn2, jnp.where(chip == 2, dn1, up3)))
+        pieces = [centroids, near, mid, far]
+    else:
+        pieces = [centroids]
+        for d in range(1, n_chip):
+            moves = [(k, (k + d) % n_chip) for k in range(n_chip)]
+            pieces.append(over_chips(centroids, moves))
     swap = [(b, b ^ 1) for b in range(n_blk)]
     swapped = [lax.ppermute(p, "blk", swap) for p in pieces]
     return jnp.concatenate(pieces + swapped, axis=0)
@@ -149,7 +166,10 @@
     first = soft_part(jnp.concatenate(arrived[1:], axis=0), part, final=True)
     ret = {d: _shift(first[(d - 1) * cap:d * cap], "cell", loops, -d) for d in range(1, loops)}
     ret[0] = soft_part(arrived[0], part, final=True)
-    mine = jnp.concatenate([ret[d] for d in range(loops)], axis=0)[slots]
+    back = jnp.concatenate([ret[d] for d in range(loops)], axis=0)
+    pick = slots[:, None] == jnp.arange(back.shape[0], dtype=jnp.int32)[None, :]
+    mine = jnp.dot(pick.astype(jnp.bfloat16), back, preferred_element_type=jnp.float32)
+    mine = mine.astype(jnp.bfloat16)
     residual = (dequant.astype(jnp.float32) - mine.astype(jnp.float32)).astype(jnp.bfloat16)
     return (mine, residual)
 

time: 50.6 us -> 55.5 us (1.097)
  starting transfers between devices: 15.6 us -> 19.8 us
  local copies, waits for them, and re-layouts: 2.82 us -> 1.37 us
  matrix products: 0 us -> 1.21 us
  waiting for transfers between devices: 11.5 us -> 12.7 us
    ppermute x3 -> x6, starting transfers between devices: 7.04 us -> 10.8 us  [over_chips(): lax.ppermute(x, 'blk', [(k * 2 + c, j * 2 + c) for k, j in moves for c in...]
    gather x1 -> x0, local copies, waits for them, and re-layouts: 1.34 us -> none  [_local(): mine = jnp.concatenate([ret[d] for d in range(loops)], axis=0)[slots]]
    dot_general x0 -> x1, matrix products: none -> 1.21 us  [_local(): jnp.dot(pick.astype(jnp.bfloat16), back, preferred_element_type=jnp.float32)]
    ppermute x6, waiting for transfers between devices: 1.34 us -> 2.27 us  [_shift(): return lax.ppermute(x, axis, [(i, (i + d) % n) for i in range(n)])]
    convert_element_type x1 -> x0, other arithmetic: 0.79 us -> none  [_local(): (dequant.astype(jnp.float32) - mine.astype(jnp.float32)).astype(jnp.bfloa...]
    ppermute x3 -> x6, waiting for transfers between devices: 8.85 us -> 9.04 us  [over_chips(): lax.ppermute(x, 'blk', [(k * 2 + c, j * 2 + c) for k, j in moves for c in...]
    unnamed x13 -> x8, local copies, waits for them, and re-layouts: 1.19 us -> 1.09 us
  transfers between devices with their start and end apart: 13 -> 16, of which waited for: 6 -> 5; matrix products, arithmetic and copies ran while one was open for 14% -> 14% of each run, Pallas kernels for 7% -> 7%
where the time goes in v2:
time: 55.5 us; the launch traced here: 55.2 us
  starting transfers between devices  19.8 us (36%)
  Pallas kernels  12.9 us (23%)
  waiting for transfers between devices  12.7 us (23%)
  other arithmetic  6.28 us (11%)
  local copies, waits for them, and re-layouts  1.37 us (2%)
  matrix products  1.21 us (2%)
  between operations  0.9 us (2%)
    pallas_call x2, Pallas kernels, soft_part(): pl.pallas_call(functools.partial(_soft_kernel, chunk=chunk, beta=1.0 / ma...  12.9 us
    ppermute x6, starting transfers between devices, over_chips(): lax.ppermute(x, 'blk', [(k * 2 + c, j * 2 + c) for k, j in moves for c in...  10.8 us
    ppermute x6, waiting for transfers between devices, over_chips(): lax.ppermute(x, 'blk', [(k * 2 + c, j * 2 + c) for k, j in moves for c in...  9.04 us
    ppermute x6, starting transfers between devices, _shift(): return lax.ppermute(x, axis, [(i, (i + d) % n) for i in range(n)])  8.21 us
    scatter x1, other arithmetic, _local(): jnp.zeros((loops * cap, width), jnp.bfloat16).at[slots].set(dequant)  2.28 us
    ppermute x6, waiting for transfers between devices, _shift(): return lax.ppermute(x, axis, [(i, (i + d) % n) for i in range(n)])  2.27 us
    another operation x2, other arithmetic  1.39 us
    ppermute x4, waiting for transfers between devices, _gather_partition(): swapped = [lax.ppermute(p, 'blk', swap) for p in pieces]  1.37 us
  transfers between devices with their start and end apart: 16, of which 5 were waited for; matrix products, arithmetic and copies ran while one was open for 14% of the time, Pallas kernels for 7%

profile of v2, /device:TPU:0, one launch (start us, length us, event | category | flops | bytes accessed | tf_op | source)
XLA Modules:
  0.0 55.2 jit_solution(10876616367816513583)
XLA Ops:
  0.6 1.3 %collective-permute-start = (bf16[1024,128]{1,0:T(8,128)(2,1)}, bf16[1024,128]{1,0:T(8,128)(2,1)S(1)}, u32[]{:S(2)}, u32[]{:S(2)}) collective-permute-start(bf16[1024,128]{1,0:T(8,128)(2,1)} %param.7), channel_id=1, source_target_pairs={{2,0},{3,1},{4,2},{5,3},{6,4},{7,5},{10,8},{11,9},{12,10},{13,11},... | collective-permute-start | bytes 786440 | tf_op jit(solution)/shard_map/ppermute | solution.py:129
  1.9 5.6 %collective-permute-start.1 = (bf16[1024,128]{1,0:T(8,128)(2,1)}, bf16[1024,128]{1,0:T(8,128)(2,1)S(1)}, u32[]{:S(2)}, u32[]{:S(2)}) collective-permute-start(bf16[1024,128]{1,0:T(8,128)(2,1)} %param.7), channel_id=1, source_target_pairs={{0,2},{1,3},{2,4},{3,5},{4,6},{5,7},{8,10},{9,11},{10,12},{11,13},... | collective-permute-start | bytes 786440 | tf_op jit(solution)/shard_map/ppermute | solution.py:129
  7.5 0.7 %fusion.14 = s32[4,4,128]{2,1,0:T(4,128)S(1)} fusion(s32[4,128]{1,0:T(4,128)} %bitcast.16), kind=kLoop, calls=%fused_computation.35 | loop fusion | flops 4096 | bytes 10240 | tf_op jit(solution)/shard_map/convert_element_type | solution.py:159
  8.2 1.2 %reduce-window.6 = s32[4,4,128]{2,1,0:T(4,128)S(1)} reduce-window(s32[4,4,128]{2,1,0:T(4,128)S(1)} %fusion.14, s32[]{:T(128)} %constant.42.clone.1), window={size=1x1x128 pad=0_0x0_0x127_0}, to_apply=%region_0.0 | reduce-window | flops 260096 | bytes 16388 | tf_op jit(solution)/shard_map/reduce-window
  9.4 0.2 slice_reduce_fusion
  9.7 0.2 reduce-window.9
  9.8 0.1 add_bitcast_fusion
  9.9 0.7 %fusion.13 = s32[512]{0:T(512)S(1)} fusion(s32[1,4,4,128]{3,2,1,0:T(4,128)S(1)} %add_bitcast_fusion, s32[512]{0:T(512)} %param.6), kind=kLoop, calls=%fused_computation.30 | loop fusion | flops 5632 | bytes 12288 | tf_op jit(solution)/shard_map/reduce_sum | solution.py:160
  10.6 0.7 %compare_select_fusion = (s32[512]{0:T(512)S(1)}, s32[512]{0:T(512)S(1)}) fusion(s32[512]{0:T(512)S(1)} %fusion.13, s32[512]{0:T(512)} %param.6, s32[]{:T(128)S(6)} %axis_index.23), kind=kLoop, calls=%fused_computation.36 | loop fusion | flops 9216 | bytes 8196 | tf_op jit(solution)/shard_map/select_n | solution.py:162
  11.3 2.3 %scatter_custom_fusion = bf16[1024,128]{1,0:T(8,128)(2,1)S(1)} fusion(s32[512]{0:T(512)S(1)} %get-tuple-element.8, bf16[]{:T(256)} %constant.47.clone.1, bf16[512,128]{1,0:T(8,128)(2,1)} %param.4, f32[512]{0:T(512)} %param.5), kind=kCustom, calls=%fused_computation.18 | custom fusion | flops 196608 | bytes 395266 | tf_op jit(solution)/shard_map/scatter | solution.py:162
  13.6 0.0 collective-permute-done
  13.6 1.3 %collective-permute-start.2 = (bf16[1024,128]{1,0:T(8,128)(2,1)S(1)}, bf16[1024,128]{1,0:T(8,128)(2,1)S(1)}, u32[]{:S(2)}, u32[]{:S(2)}) collective-permute-start(bf16[1024,128]{1,0:T(8,128)(2,1)S(1)} %collective-permute-done), channel_id=1, source_target_pairs={{4,2},{5,3},{2,0},{3,1},{12,10},{13,11},{10,8},{11,9},{20,18},{21,... | collective-permute-start | bytes 786440 | tf_op jit(solution)/shard_map/ppermute | solution.py:129
  14.9 0.0 collective-permute-done.1
  14.9 0.7 %collective-permute-start.3 = (bf16[1024,128]{1,0:T(8,128)(2,1)S(1)}, bf16[1024,128]{1,0:T(8,128)(2,1)S(1)}, u32[]{:S(2)}, u32[]{:S(2)}) collective-permute-start(bf16[1024,128]{1,0:T(8,128)(2,1)S(1)} %collective-permute-done.1), channel_id=1, source_target_pairs={{2,4},{3,5},{4,6},{5,7},{10,12},{11,13},{12,14},{13,15},{18,20},{1... | collective-permute-start | bytes 786440 | tf_op jit(solution)/shard_map/ppermute | solution.py:129
  15.6 2.0 %collective-permute-start.10 = (bf16[256,128]{1,0:T(8,128)(2,1)S(1)}, bf16[256,128]{1,0:T(8,128)(2,1)S(1)}, u32[]{:S(2)}, u32[]{:S(2)}) collective-permute-start(bf16[256,128]{1,0:T(8,128)(2,1)S(1)} %get-tuple-element.13), channel_id=1, source_target_pairs={{0,8},{8,16},{16,24},{24,0},{1,9},{9,17},{17,25},{25,1},{2,10},{10... | collective-permute-start | bytes 196616 | tf_op jit(solution)/shard_map/ppermute | solution.py:120
  17.6 1.5 %collective-permute-start.11 = (bf16[256,128]{1,0:T(8,128)(2,1)S(1)}, bf16[256,128]{1,0:T(8,128)(2,1)S(1)}, u32[]{:S(2)}, u32[]{:S(2)}) collective-permute-start(bf16[256,128]{1,0:T(8,128)(2,1)S(1)} %get-tuple-element.12), channel_id=1, source_target_pairs={{0,16},{8,24},{16,0},{24,8},{1,17},{9,25},{17,1},{25,9},{2,18},{10... | collective-permute-start | bytes 196616 | tf_op jit(solution)/shard_map/ppermute | solution.py:120
  19.1 1.4 %collective-permute-start.12 = (bf16[256,128]{1,0:T(8,128)(2,1)S(1)}, bf16[256,128]{1,0:T(8,128)(2,1)S(1)}, u32[]{:S(2)}, u32[]{:S(2)}) collective-permute-start(bf16[256,128]{1,0:T(8,128)(2,1)S(1)} %get-tuple-element.11), channel_id=1, source_target_pairs={{0,24},{8,0},{16,8},{24,16},{1,25},{9,1},{17,9},{25,17},{2,26},{10... | collective-permute-start | bytes 196616 | tf_op jit(solution)/shard_map/ppermute | solution.py:120
  20.6 1.0 %constant_dynamic-update-slice_fusion.7 = bf16[8192,128]{1,0:T(8,128)(2,1)S(1)} fusion(bf16[1024,128]{1,0:T(8,128)(2,1)} %param.7), kind=kLoop, calls=%fused_computation.27 | loop fusion | bytes 524288
  21.6 0.0 collective-permute-done.10
  21.6 0.1 collective-permute-start.6
  21.6 0.3 collective-permute-done.11
  22.0 1.5 %collective-permute-done.12 = bf16[256,128]{1,0:T(8,128)(2,1)S(1)} collective-permute-done((bf16[256,128]{1,0:T(8,128)(2,1)S(1)}, bf16[256,128]{1,0:T(8,128)(2,1)S(1)}, u32[]{:S(2)}, u32[]{:S(2)}) %collective-permute-start.12) | collective-permute-done | bytes 65568 | tf_op jit(solution)/shard_map/ppermute | solution.py:120
  23.4 0.0 collective-permute-done.2
  23.4 1.3 %collective-permute-start.4 = (bf16[1024,128]{1,0:T(8,128)(2,1)S(1)}, bf16[1024,128]{1,0:T(8,128)(2,1)S(1)}, u32[]{:S(2)}, u32[]{:S(2)}) collective-permute-start(bf16[1024,128]{1,0:T(8,128)(2,1)S(1)} %collective-permute-done.2), channel_id=1, source_target_pairs={{2,0},{3,1},{10,8},{11,9},{18,16},{19,17},{26,24},{27,25}} | collective-permute-start | bytes 786440 | tf_op jit(solution)/shard_map/ppermute | solution.py:129
  24.7 0.0 collective-permute-done.3
  24.8 0.7 %collective-permute-start.5 = (bf16[1024,128]{1,0:T(8,128)(2,1)S(1)}, bf16[1024,128]{1,0:T(8,128)(2,1)S(1)}, u32[]{:S(2)}, u32[]{:S(2)}) collective-permute-start(bf16[1024,128]{1,0:T(8,128)(2,1)S(1)} %collective-permute-done.3), channel_id=1, source_target_pairs={{4,6},{5,7},{12,14},{13,15},{20,22},{21,23},{28,30},{29,31}} | collective-permute-start | bytes 786440 | tf_op jit(solution)/shard_map/ppermute | solution.py:129
  25.4 0.1 constant_dynamic-update-slice_fusion.6
  25.6 0.1 collective-permute-start.7
  25.6 0.1 constant_dynamic-update-slice_fusion.5
  25.8 0.6 %collective-permute-start.8 = (bf16[1024,128]{1,0:T(8,128)(2,1)S(1)}, bf16[1024,128]{1,0:T(8,128)(2,1)S(1)}, u32[]{:S(2)}, u32[]{:S(2)}) collective-permute-start(bf16[1024,128]{1,0:T(8,128)(2,1)S(1)} %get-tuple-element.5), channel_id=1, source_target_pairs={{0,1},{1,0},{2,3},{3,2},{4,5},{5,4},{6,7},{7,6},{8,9},{9,8},{10,11... | collective-permute-start | bytes 786440 | tf_op jit(solution)/shard_map/ppermute | solution.py:148
  26.3 9.0 %collective-permute-done.4 = bf16[1024,128]{1,0:T(8,128)(2,1)S(1)} collective-permute-done((bf16[1024,128]{1,0:T(8,128)(2,1)S(1)}, bf16[1024,128]{1,0:T(8,128)(2,1)S(1)}, u32[]{:S(2)}, u32[]{:S(2)}) %collective-permute-start.4) | collective-permute-done | bytes 262176 | tf_op jit(solution)/shard_map/ppermute | solution.py:129
  35.4 0.0 collective-permute-done.5
  35.4 0.2 constant_dynamic-update-slice_fusion.4
  35.6 0.1 collective-permute-start.9
  35.6 0.0 collective-permute-done.6
  35.7 0.0 collective-permute-done.7
  35.7 0.0 collective-permute-done.8
  35.8 1.4 %collective-permute-done.9 = bf16[1024,128]{1,0:T(8,128)(2,1)S(1)} collective-permute-done((bf16[1024,128]{1,0:T(8,128)(2,1)S(1)}, bf16[1024,128]{1,0:T(8,128)(2,1)S(1)}, u32[]{:S(2)}, u32[]{:S(2)}) %collective-permute-start.9) | collective-permute-done | bytes 262176 | tf_op jit(solution)/shard_map/ppermute | solution.py:148
  37.2 9.2 %shard_map.60 = bf16[768,128]{1,0:T(8,128)(2,1)S(1)} custom-call(bf16[768,128]{1,0:T(8,128)(2,1)S(1)} %pad_maximum_fusion.refs_0_, bf16[8192,128]{1,0:T(8,128)(2,1)S(1)} %constant_dynamic-update-slice_fusion.refs_1_), custom_call_target="tpu_custom_call" | custom-call | flops 3221225472 | bytes 2490368 | tf_op jit(solution)/shard_map/pallas_call | solution.py:92
  46.4 0.0 copy-start
  46.4 0.0 copy-start.1
  46.5 1.5 %collective-permute-start.13 = (bf16[256,128]{1,0:T(8,128)(2,1)S(1)}, bf16[256,128]{1,0:T(8,128)(2,1)S(1)}, u32[]{:S(2)}, u32[]{:S(2)}) collective-permute-start(bf16[256,128]{1,0:T(8,128)(2,1)S(1)} %get-tuple-element.14), channel_id=1, source_target_pairs={{0,24},{8,0},{16,8},{24,16},{1,25},{9,1},{17,9},{25,17},{2,26},{10... | collective-permute-start | bytes 196616 | tf_op jit(solution)/shard_map/ppermute | solution.py:120
  48.0 0.8 %collective-permute-start.14 = (bf16[256,128]{1,0:T(8,128)(2,1)S(1)}, bf16[256,128]{1,0:T(8,128)(2,1)S(1)}, u32[]{:S(2)}, u32[]{:S(2)}) collective-permute-start(bf16[256,128]{1,0:T(8,128)(2,1)S(1)} %get-tuple-element.16), channel_id=1, source_target_pairs={{0,16},{8,24},{16,0},{24,8},{1,17},{9,25},{17,1},{25,9},{2,18},{10... | collective-permute-start | bytes 196616 | tf_op jit(solution)/shard_map/ppermute | solution.py:120
  48.8 0.9 %collective-permute-start.15 = (bf16[256,128]{1,0:T(8,128)(2,1)S(1)}, bf16[256,128]{1,0:T(8,128)(2,1)S(1)}, u32[]{:S(2)}, u32[]{:S(2)}) collective-permute-start(bf16[256,128]{1,0:T(8,128)(2,1)S(1)} %get-tuple-element.15), channel_id=1, source_target_pairs={{0,8},{8,16},{16,24},{24,0},{1,9},{9,17},{17,25},{25,1},{2,10},{10... | collective-permute-start | bytes 196616 | tf_op jit(solution)/shard_map/ppermute | solution.py:120
  49.8 3.7 %shard_map.59 = bf16[256,128]{1,0:T(8,128)(2,1)S(1)} custom-call(bf16[256,128]{1,0:T(8,128)(2,1)S(1)} %get-tuple-element.10.refs_0_, bf16[8192,128]{1,0:T(8,128)(2,1)S(1)} %constant_dynamic-update-slice_fusion.refs_1_), custom_call_target="tpu_custom_call" | custom-call | flops 1073741824 | bytes 2228224 | tf_op jit(solution)/shard_map/pallas_call | solution.py:92
  53.5 0.0 collective-permute-done.13
  53.5 0.0 collective-permute-done.14
  53.5 0.5 collective-permute-done.15
  54.0 0.0 copy-done
  54.0 0.0 copy-done.1
  54.0 1.2 %subtract_convert_fusion = (bf16[512,128]{1,0:T(8,128)(2,1)}, bf16[512,128]{1,0:T(8,128)(2,1)}) fusion(f32[512]{0:T(512)S(1)} %copy-done.1, bf16[512,128]{1,0:T(8,128)(2,1)S(1)} %copy-done, bf16[256,128]{1,0:T(8,128)(2,1)S(1)} %collective-permute-done.15, bf16[256,128]{1,0:T(8,128)(2,1)S(1)} %collective-permute-done.14, ...), kind=kOutput, calls=%fused_computation.12 | convolution fusion | flops 136314880 | bytes 659456 | tf_op jit(solution)/shard_map/dot_general | solution.py:171
  (7 shorter events, 0.2 us)
Async XLA Ops:
  0.6 13.0 %collective-permute-start = (bf16[1024,128]{1,0:T(8,128)(2,1)}, bf16[1024,128]{1,0:T(8,128)(2,1)S(1)}, u32[]{:S(2)}, u32[]{:S(2)}) collective-permute-start(bf16[1024,128]{1,0:T(8,128)(2,1)} %param.7), channel_id=1, source_target_pairs={{2,0},{3,1},{4,2},{5,3},{6,4},{7,5},{10,8},{11,9},{12,10},{13,11},... | collective-permute-start | bytes 786440 | tf_op jit(solution)/shard_map/ppermute | solution.py:129
  1.9 13.0 %collective-permute-start.1 = (bf16[1024,128]{1,0:T(8,128)(2,1)}, bf16[1024,128]{1,0:T(8,128)(2,1)S(1)}, u32[]{:S(2)}, u32[]{:S(2)}) collective-permute-start(bf16[1024,128]{1,0:T(8,128)(2,1)} %param.7), channel_id=1, source_target_pairs={{0,2},{1,3},{2,4},{3,5},{4,6},{5,7},{8,10},{9,11},{10,12},{11,13},... | collective-permute-start | bytes 786440 | tf_op jit(solution)/shard_map/ppermute | solution.py:129
  13.6 9.8 %collective-permute-start.2 = (bf16[1024,128]{1,0:T(8,128)(2,1)S(1)}, bf16[1024,128]{1,0:T(8,128)(2,1)S(1)}, u32[]{:S(2)}, u32[]{:S(2)}) collective-permute-start(bf16[1024,128]{1,0:T(8,128)(2,1)S(1)} %collective-permute-done), channel_id=1, source_target_pairs={{4,2},{5,3},{2,0},{3,1},{12,10},{13,11},{10,8},{11,9},{20,18},{21,... | collective-permute-start | bytes 786440 | tf_op jit(solution)/shard_map/ppermute | solution.py:129
  14.9 9.8 %collective-permute-start.3 = (bf16[1024,128]{1,0:T(8,128)(2,1)S(1)}, bf16[1024,128]{1,0:T(8,128)(2,1)S(1)}, u32[]{:S(2)}, u32[]{:S(2)}) collective-permute-start(bf16[1024,128]{1,0:T(8,128)(2,1)S(1)} %collective-permute-done.1), channel_id=1, source_target_pairs={{2,4},{3,5},{4,6},{5,7},{10,12},{11,13},{12,14},{13,15},{18,20},{1... | collective-permute-start | bytes 786440 | tf_op jit(solution)/shard_map/ppermute | solution.py:129
  15.6 5.9 %collective-permute-start.10 = (bf16[256,128]{1,0:T(8,128)(2,1)S(1)}, bf16[256,128]{1,0:T(8,128)(2,1)S(1)}, u32[]{:S(2)}, u32[]{:S(2)}) collective-permute-start(bf16[256,128]{1,0:T(8,128)(2,1)S(1)} %get-tuple-element.13), channel_id=1, source_target_pairs={{0,8},{8,16},{16,24},{24,0},{1,9},{9,17},{17,25},{25,1},{2,10},{10... | collective-permute-start | bytes 196616 | tf_op jit(solution)/shard_map/ppermute | solution.py:120
  17.6 4.3 %collective-permute-start.11 = (bf16[256,128]{1,0:T(8,128)(2,1)S(1)}, bf16[256,128]{1,0:T(8,128)(2,1)S(1)}, u32[]{:S(2)}, u32[]{:S(2)}) collective-permute-start(bf16[256,128]{1,0:T(8,128)(2,1)S(1)} %get-tuple-element.12), channel_id=1, source_target_pairs={{0,16},{8,24},{16,0},{24,8},{1,17},{9,25},{17,1},{25,9},{2,18},{10... | collective-permute-start | bytes 196616 | tf_op jit(solution)/shard_map/ppermute | solution.py:120
  19.1 4.3 %collective-permute-start.12 = (bf16[256,128]{1,0:T(8,128)(2,1)S(1)}, bf16[256,128]{1,0:T(8,128)(2,1)S(1)}, u32[]{:S(2)}, u32[]{:S(2)}) collective-permute-start(bf16[256,128]{1,0:T(8,128)(2,1)S(1)} %get-tuple-element.11), channel_id=1, source_target_pairs={{0,24},{8,0},{16,8},{24,16},{1,25},{9,1},{17,9},{25,17},{2,26},{10... | collective-permute-start | bytes 196616 | tf_op jit(solution)/shard_map/ppermute | solution.py:120
  21.6 14.1 %collective-permute-start.6 = (bf16[1024,128]{1,0:T(8,128)(2,1)}, bf16[1024,128]{1,0:T(8,128)(2,1)S(1)}, u32[]{:S(2)}, u32[]{:S(2)}) collective-permute-start(bf16[1024,128]{1,0:T(8,128)(2,1)} %param.7), channel_id=1, source_target_pairs={{0,1},{1,0},{2,3},{3,2},{4,5},{5,4},{6,7},{7,6},{8,9},{9,8},{10,11... | collective-permute-start | bytes 786440 | tf_op jit(solution)/shard_map/ppermute | solution.py:148
  23.4 11.9 %collective-permute-start.4 = (bf16[1024,128]{1,0:T(8,128)(2,1)S(1)}, bf16[1024,128]{1,0:T(8,128)(2,1)S(1)}, u32[]{:S(2)}, u32[]{:S(2)}) collective-permute-start(bf16[1024,128]{1,0:T(8,128)(2,1)S(1)} %collective-permute-done.2), channel_id=1, source_target_pairs={{2,0},{3,1},{10,8},{11,9},{18,16},{19,17},{26,24},{27,25}} | collective-permute-start | bytes 786440 | tf_op jit(solution)/shard_map/ppermute | solution.py:129
  24.8 10.6 %collective-permute-start.5 = (bf16[1024,128]{1,0:T(8,128)(2,1)S(1)}, bf16[1024,128]{1,0:T(8,128)(2,1)S(1)}, u32[]{:S(2)}, u32[]{:S(2)}) collective-permute-start(bf16[1024,128]{1,0:T(8,128)(2,1)S(1)} %collective-permute-done.3), channel_id=1, source_target_pairs={{4,6},{5,7},{12,14},{13,15},{20,22},{21,23},{28,30},{29,31}} | collective-permute-start | bytes 786440 | tf_op jit(solution)/shard_map/ppermute | solution.py:129
  25.6 10.1 %collective-permute-start.7 = (bf16[1024,128]{1,0:T(8,128)(2,1)S(1)}, bf16[1024,128]{1,0:T(8,128)(2,1)S(1)}, u32[]{:S(2)}, u32[]{:S(2)}) collective-permute-start(bf16[1024,128]{1,0:T(8,128)(2,1)S(1)} %get-tuple-element.7), channel_id=1, source_target_pairs={{0,1},{1,0},{2,3},{3,2},{4,5},{5,4},{6,7},{7,6},{8,9},{9,8},{10,11... | collective-permute-start | bytes 786440 | tf_op jit(solution)/shard_map/ppermute | solution.py:148
  25.8 10.0 %collective-permute-start.8 = (bf16[1024,128]{1,0:T(8,128)(2,1)S(1)}, bf16[1024,128]{1,0:T(8,128)(2,1)S(1)}, u32[]{:S(2)}, u32[]{:S(2)}) collective-permute-start(bf16[1024,128]{1,0:T(8,128)(2,1)S(1)} %get-tuple-element.5), channel_id=1, source_target_pairs={{0,1},{1,0},{2,3},{3,2},{4,5},{5,4},{6,7},{7,6},{8,9},{9,8},{10,11... | collective-permute-start | bytes 786440 | tf_op jit(solution)/shard_map/ppermute | solution.py:148
  35.6 1.6 %collective-permute-start.9 = (bf16[1024,128]{1,0:T(8,128)(2,1)S(1)}, bf16[1024,128]{1,0:T(8,128)(2,1)S(1)}, u32[]{:S(2)}, u32[]{:S(2)}) collective-permute-start(bf16[1024,128]{1,0:T(8,128)(2,1)S(1)} %get-tuple-element.3), channel_id=1, source_target_pairs={{0,1},{1,0},{2,3},{3,2},{4,5},{5,4},{6,7},{7,6},{8,9},{9,8},{10,11... | collective-permute-start | bytes 786440 | tf_op jit(solution)/shard_map/ppermute | solution.py:148
  46.4 7.6 %copy-start = (bf16[512,128]{1,0:T(8,128)(2,1)S(1)}, bf16[512,128]{1,0:T(8,128)(2,1)}, u32[]{:S(2)}) copy-start(bf16[512,128]{1,0:T(8,128)(2,1)} %param.4) | copy-start | bytes 393220
  46.4 7.5 %copy-start.1 = (f32[512]{0:T(512)S(1)}, f32[512]{0:T(512)}, u32[]{:S(2)}) copy-start(f32[512]{0:T(512)} %param.5) | copy-start | bytes 6148
  46.5 7.0 %collective-permute-start.13 = (bf16[256,128]{1,0:T(8,128)(2,1)S(1)}, bf16[256,128]{1,0:T(8,128)(2,1)S(1)}, u32[]{:S(2)}, u32[]{:S(2)}) collective-permute-start(bf16[256,128]{1,0:T(8,128)(2,1)S(1)} %get-tuple-element.14), channel_id=1, source_target_pairs={{0,24},{8,0},{16,8},{24,16},{1,25},{9,1},{17,9},{25,17},{2,26},{10... | collective-permute-start | bytes 196616 | tf_op jit(solution)/shard_map/ppermute | solution.py:120
  48.0 5.5 %collective-permute-start.14 = (bf16[256,128]{1,0:T(8,128)(2,1)S(1)}, bf16[256,128]{1,0:T(8,128)(2,1)S(1)}, u32[]{:S(2)}, u32[]{:S(2)}) collective-permute-start(bf16[256,128]{1,0:T(8,128)(2,1)S(1)} %get-tuple-element.16), channel_id=1, source_target_pairs={{0,16},{8,24},{16,0},{24,8},{1,17},{9,25},{17,1},{25,9},{2,18},{10... | collective-permute-start | bytes 196616 | tf_op jit(solution)/shard_map/ppermute | solution.py:120
  48.8 5.2 %collective-permute-start.15 = (bf16[256,128]{1,0:T(8,128)(2,1)S(1)}, bf16[256,128]{1,0:T(8,128)(2,1)S(1)}, u32[]{:S(2)}, u32[]{:S(2)}) collective-permute-start(bf16[256,128]{1,0:T(8,128)(2,1)S(1)} %get-tuple-element.15), channel_id=1, source_target_pairs={{0,8},{8,16},{16,24},{24,0},{1,9},{9,17},{17,25},{25,1},{2,10},{10... | collective-permute-start | bytes 196616 | tf_op jit(solution)/shard_map/ppermute | solution.py:120

commit v3 on v0

--- a/solution.py
+++ b/solution.py
@@ -9,7 +9,21 @@
 from jax.sharding import PartitionSpec as P
 
 
-def _soft_kernel(*refs, chunk, beta, merge, final):
+def _soft_kernel(*refs, chunk, beta, merge, final, counted=False):
+    if counted:
+        n_ref, refs = refs[0], refs[1:]
+        o_ref = refs[2]
+        live = pl.program_id(0) * o_ref.shape[0] < n_ref[0]
+
+        @pl.when(live)
+        def _():
+            _soft_kernel(*refs, chunk=chunk, beta=beta, merge=merge, final=final)
+
+        @pl.when(jnp.logical_not(live))
+        def _():
+            o_ref[...] = jnp.zeros(o_ref.shape, o_ref.dtype)
+
+        return
     if not merge and final:
         q_ref, c_ref, o_ref, m_sc, l_sc, acc_sc, s_sc = refs
     elif merge:
@@ -64,11 +78,11 @@
         oacc_ref[...] = acc_sc[...]
 
 
-def soft_part(queries, cents, prior=None, final=False):
+def soft_part(queries, cents, prior=None, final=False, count=None, tiles=1):
     slots, width = queries.shape
     n_cent = cents.shape[0]
     chunk = min(4096, n_cent)
-    tq = slots
+    tq = slots // tiles
     while tq * n_cent * 4 > (32 << 20) and tq % 16 == 0:
         tq //= 2
     vmem = 4 * tq * n_cent + 2 * 2 * n_cent * width + 16 * tq * width * 4 + (8 << 20)
@@ -89,30 +103,50 @@
         in_specs += [col, col, rows]
         out_shape = jax.ShapeDtypeStruct((slots, width), jnp.bfloat16)
         out_specs, args = rows, (queries, cents) + tuple(prior)
+    kernel = functools.partial(
+        _soft_kernel,
+        chunk=chunk,
+        beta=1.0 / math.sqrt(width),
+        merge=prior is not None,
+        final=final or prior is not None,
+        counted=count is not None,
+    )
+    scratch = [
+        pltpu.VMEM((tq, 128), jnp.float32),
+        pltpu.VMEM((tq, 128), jnp.float32),
+        pltpu.VMEM((tq, width), jnp.float32),
+        pltpu.VMEM((tq, n_cent), jnp.float32),
+    ]
+    params = pltpu.CompilerParams(vmem_limit_bytes=min(vmem, 60 << 20))
+    cost = pl.CostEstimate(
+        flops=2 * 2 * slots * n_cent * width,
+        transcendentals=slots * n_cent,
+        bytes_accessed=2 * (2 * slots * width + n_cent * width),
+    )
+    if count is not None:
+        grid_spec = pltpu.PrefetchScalarGridSpec(
+            num_scalar_prefetch=1,
+            grid=(slots // tq,),
+            in_specs=[
+                pl.BlockSpec((tq, width), lambda i, n: (i, 0)),
+                pl.BlockSpec((n_cent, width), lambda i, n: (0, 0)),
+            ],
+            out_specs=pl.BlockSpec((tq, width), lambda i, n: (i, 0)),
+            scratch_shapes=scratch,
+        )
+        return pl.pallas_call(
+            kernel, out_shape=out_shape, grid_spec=grid_spec, compiler_params=params,
+            cost_estimate=cost,
+        )(count, *args)
     return pl.pallas_call(
-        functools.partial(
-            _soft_kernel,
-            chunk=chunk,
-            beta=1.0 / math.sqrt(width),
-            merge=prior is not None,
-            final=final or prior is not None,
-        ),
+        kernel,
         out_shape=out_shape,
         grid=(slots // tq,),
         in_specs=in_specs,
         out_specs=out_specs,
-        scratch_shapes=[
-            pltpu.VMEM((tq, 128), jnp.float32),
-            pltpu.VMEM((tq, 128), jnp.float32),
-            pltpu.VMEM((tq, width), jnp.float32),
-            pltpu.VMEM((tq, n_cent), jnp.float32),
-        ],
-        compiler_params=pltpu.CompilerParams(vmem_limit_bytes=min(vmem, 60 << 20)),
-        cost_estimate=pl.CostEstimate(
-            flops=2 * 2 * slots * n_cent * width,
-            transcendentals=slots * n_cent,
-            bytes_accessed=2 * (2 * slots * width + n_cent * width),
-        ),
+        scratch_shapes=scratch,
+        compiler_params=params,
+        cost_estimate=cost,
     )(*args)
 
 
@@ -146,10 +180,17 @@
     outgoing = outgoing.reshape(loops, cap, width)
     part = _gather_partition(centroids)
     arrived = [outgoing[0]] + [_shift(outgoing[d], "cell", loops, d) for d in range(1, loops)]
-    first = soft_part(jnp.concatenate(arrived[1:], axis=0), part, final=True)
-    ret = {d: _shift(first[(d - 1) * cap:d * cap], "cell", loops, -d) for d in range(1, loops)}
+    real = jnp.sum((coarse_ids == me).astype(jnp.int32))
+    remote = jnp.stack(arrived[1:], axis=1).reshape((loops - 1) * cap, width)
+    count = ((loops - 1) * real).reshape(1)
+    first = soft_part(remote, part, final=True, count=count, tiles=2)
+    first = first.reshape(cap, loops - 1, width)
+    ret = {d: _shift(first[:, d - 1], "cell", loops, -d) for d in range(1, loops)}
     ret[0] = soft_part(arrived[0], part, final=True)
-    mine = jnp.concatenate([ret[d] for d in range(loops)], axis=0)[slots]
+    back = jnp.concatenate([ret[d] for d in range(loops)], axis=0)
+    pick = slots[:, None] == jnp.arange(back.shape[0], dtype=jnp.int32)[None, :]
+    mine = jnp.dot(pick.astype(jnp.bfloat16), back, preferred_element_type=jnp.float32)
+    mine = mine.astype(jnp.bfloat16)
     residual = (dequant.astype(jnp.float32) - mine.astype(jnp.float32)).astype(jnp.bfloat16)
     return (mine, residual)
 

time: 50.6 us -> 51.8 us (1.024)
  starting transfers between devices: 15.6 us -> 20.3 us
  Pallas kernels: 12.9 us -> 8.81 us
  waiting for transfers between devices: 11.5 us -> 9.06 us
  local copies, waits for them, and re-layouts: 2.82 us -> 4.1 us
  matrix products: 0 us -> 1.21 us
  between operations: 0.82 us -> 1.5 us
    ppermute x6, starting transfers between devices: 8.09 us -> 12.6 us  [_shift(): return lax.ppermute(x, axis, [(i, (i + d) % n) for i in range(n)])]
    pallas_call x2, Pallas kernels: 12.9 us -> 8.81 us  [the longest x1 5.1 us: soft_part(): pl.pallas_call(kernel, out_shape=out_shape, grid_spec=grid_spec, compiler...]
    unnamed x13 -> x14, local copies, waits for them, and re-layouts: 1.19 us -> 3.13 us
    gather x1 -> x0, local copies, waits for them, and re-layouts: 1.34 us -> none  [_local(): mine = jnp.concatenate([ret[d] for d in range(loops)], axis=0)[slots]]
    ppermute x4, waiting for transfers between devices: 1.32 us -> 0.01 us  [_gather_partition(): swapped = [lax.ppermute(p, 'blk', swap) for p in pieces]]
    ppermute x3, waiting for transfers between devices: 8.85 us -> 7.63 us  [_gather_partition(): pieces.append(lax.ppermute(centroids, 'blk', pairs))]
    dot_general x0 -> x1, matrix products: none -> 1.21 us  [_local(): jnp.dot(pick.astype(jnp.bfloat16), back, preferred_element_type=jnp.float32)]
    convert_element_type x1 -> x0, other arithmetic: 0.79 us -> none  [_local(): (dequant.astype(jnp.float32) - mine.astype(jnp.float32)).astype(jnp.bfloa...]
  transfers between devices with their start and end apart: 13 -> 13, of which waited for: 6 -> 3; matrix products, arithmetic and copies ran while one was open for 14% -> 20% of each run, Pallas kernels for 7% -> 7%
where the time goes in v3:
time: 51.8 us; the launch traced here: 51.5 us
  starting transfers between devices  20.3 us (39%)
  waiting for transfers between devices  9.06 us (17%)
  Pallas kernels  8.81 us (17%)
  other arithmetic  6.49 us (13%)
  local copies, waits for them, and re-layouts  4.1 us (8%)
  between operations  1.5 us (3%)
  matrix products  1.21 us (2%)
    ppermute x6, starting transfers between devices, _shift(): return lax.ppermute(x, axis, [(i, (i + d) % n) for i in range(n)])  12.6 us
    ppermute x3, waiting for transfers between devices, _gather_partition(): pieces.append(lax.ppermute(centroids, 'blk', pairs))  7.63 us
    ppermute x3, starting transfers between devices, _gather_partition(): pieces.append(lax.ppermute(centroids, 'blk', pairs))  7.1 us
    pallas_call x1, Pallas kernels, soft_part(): pl.pallas_call(kernel, out_shape=out_shape, grid_spec=grid_spec, compiler...  5.1 us
    pallas_call x1, Pallas kernels, soft_part(): pl.pallas_call(kernel, out_shape=out_shape, grid=(slots // tq,), in_specs...  3.71 us
    unnamed x14, local copies, waits for them, and re-layouts  3.13 us
    scatter x1, other arithmetic, _local(): jnp.zeros((loops * cap, width), jnp.bfloat16).at[slots].set(dequant)  2.28 us
    ppermute x6, waiting for transfers between devices, _shift(): return lax.ppermute(x, axis, [(i, (i + d) % n) for i in range(n)])  1.43 us
  transfers between devices with their start and end apart: 13, of which 3 were waited for; matrix products, arithmetic and copies ran while one was open for 20% of the time, Pallas kernels for 7%

profile of v3, /device:TPU:0, one launch (start us, length us, event | category | flops | bytes accessed | tf_op | source)
XLA Modules:
  0.0 51.5 jit_solution(823690746966877504)
XLA Ops:
  0.6 3.1 %collective-permute-start = (bf16[1024,128]{1,0:T(8,128)(2,1)}, bf16[1024,128]{1,0:T(8,128)(2,1)S(1)}, u32[]{:S(2)}, u32[]{:S(2)}) collective-permute-start(bf16[1024,128]{1,0:T(8,128)(2,1)} %param.7), channel_id=1, source_target_pairs={{0,2},{1,3},{2,4},{3,5},{4,6},{5,7},{6,0},{7,1},{8,10},{9,11},{10,... | collective-permute-start | bytes 786440 | tf_op jit(solution)/shard_map/ppermute | solution.py:163
  3.7 2.6 %collective-permute-start.1 = (bf16[1024,128]{1,0:T(8,128)(2,1)}, bf16[1024,128]{1,0:T(8,128)(2,1)S(1)}, u32[]{:S(2)}, u32[]{:S(2)}) collective-permute-start(bf16[1024,128]{1,0:T(8,128)(2,1)} %param.7), channel_id=1, source_target_pairs={{0,4},{1,5},{2,6},{3,7},{4,0},{5,1},{6,2},{7,3},{8,12},{9,13},{10,... | collective-permute-start | bytes 786440 | tf_op jit(solution)/shard_map/ppermute | solution.py:163
  6.3 0.7 %fusion.14 = s32[4,4,128]{2,1,0:T(4,128)S(1)} fusion(s32[4,128]{1,0:T(4,128)} %bitcast.35), kind=kLoop, calls=%fused_computation.35 | loop fusion | flops 4096 | bytes 10240 | tf_op jit(solution)/shard_map/convert_element_type | solution.py:176
  7.0 1.2 %reduce-window.6 = s32[4,4,128]{2,1,0:T(4,128)S(1)} reduce-window(s32[4,4,128]{2,1,0:T(4,128)S(1)} %fusion.14, s32[]{:T(128)} %constant.29.clone.1), window={size=1x1x128 pad=0_0x0_0x127_0}, to_apply=%region_0.0 | reduce-window | flops 260096 | bytes 16388 | tf_op jit(solution)/shard_map/reduce-window
  8.2 0.2 slice_reduce_fusion
  8.4 0.2 reduce-window.9
  8.6 0.1 add_bitcast_fusion
  8.7 0.7 %fusion.13 = s32[512]{0:T(512)S(1)} fusion(s32[1,4,4,128]{3,2,1,0:T(4,128)S(1)} %add_bitcast_fusion, s32[512]{0:T(512)} %param.6), kind=kLoop, calls=%fused_computation.30 | loop fusion | flops 5632 | bytes 12288 | tf_op jit(solution)/shard_map/reduce_sum | solution.py:177
  9.4 1.3 %compare_select_fusion = (s32[512]{0:T(512)S(1)}, s32[512]{0:T(512)S(1)}, s32[]{:T(128)}) fusion(s32[512]{0:T(512)S(1)} %fusion.13, s32[512]{0:T(512)} %param.6, s32[]{:T(128)S(6)} %axis_index.15), kind=kLoop, calls=%fused_computation.36 | loop fusion | flops 10751 | bytes 8200 | tf_op jit(solution)/shard_map/select_n | solution.py:179
  10.7 2.3 %scatter_custom_fusion = bf16[1024,128]{1,0:T(8,128)(2,1)S(1)} fusion(s32[512]{0:T(512)S(1)} %get-tuple-element.2, bf16[]{:T(256)} %constant.34.clone.1, bf16[512,128]{1,0:T(8,128)(2,1)} %param.4, f32[512]{0:T(512)} %param.5), kind=kCustom, calls=%fused_computation.15 | custom fusion | flops 196608 | bytes 395266 | tf_op jit(solution)/shard_map/scatter | solution.py:179
  13.0 1.5 %collective-permute-start.7 = (bf16[256,128]{1,0:T(8,128)(2,1)S(1)}, bf16[256,128]{1,0:T(8,128)(2,1)S(1)}, u32[]{:S(2)}, u32[]{:S(2)}) collective-permute-start(bf16[256,128]{1,0:T(8,128)(2,1)S(1)} %get-tuple-element.7), channel_id=1, source_target_pairs={{0,8},{8,16},{16,24},{24,0},{1,9},{9,17},{17,25},{25,1},{2,10},{10... | collective-permute-start | bytes 196616 | tf_op jit(solution)/shard_map/ppermute | solution.py:154
  14.6 1.5 %collective-permute-start.8 = (bf16[256,128]{1,0:T(8,128)(2,1)S(1)}, bf16[256,128]{1,0:T(8,128)(2,1)S(1)}, u32[]{:S(2)}, u32[]{:S(2)}) collective-permute-start(bf16[256,128]{1,0:T(8,128)(2,1)S(1)} %get-tuple-element.6), channel_id=1, source_target_pairs={{0,16},{8,24},{16,0},{24,8},{1,17},{9,25},{17,1},{25,9},{2,18},{10... | collective-permute-start | bytes 196616 | tf_op jit(solution)/shard_map/ppermute | solution.py:154
  16.1 1.4 %collective-permute-start.9 = (bf16[256,128]{1,0:T(8,128)(2,1)S(1)}, bf16[256,128]{1,0:T(8,128)(2,1)S(1)}, u32[]{:S(2)}, u32[]{:S(2)}) collective-permute-start(bf16[256,128]{1,0:T(8,128)(2,1)S(1)} %get-tuple-element.5), channel_id=1, source_target_pairs={{0,24},{8,0},{16,8},{24,16},{1,25},{9,1},{17,9},{25,17},{2,26},{10... | collective-permute-start | bytes 196616 | tf_op jit(solution)/shard_map/ppermute | solution.py:154
  17.5 1.0 %constant_dynamic-update-slice_fusion.7 = bf16[8192,128]{1,0:T(8,128)(2,1)S(1)} fusion(bf16[1024,128]{1,0:T(8,128)(2,1)} %param.7), kind=kLoop, calls=%fused_computation.27 | loop fusion | bytes 524288
  19.2 0.0 collective-permute-done.7
  19.2 1.4 %collective-permute-start.2 = (bf16[1024,128]{1,0:T(8,128)(2,1)}, bf16[1024,128]{1,0:T(8,128)(2,1)}, u32[]{:S(2)}, u32[]{:S(2)}) collective-permute-start(bf16[1024,128]{1,0:T(8,128)(2,1)} %param.7), channel_id=1, source_target_pairs={{0,6},{1,7},{2,0},{3,1},{4,2},{5,3},{6,4},{7,5},{8,14},{9,15},{10,... | collective-permute-start | bytes 786440 | tf_op jit(solution)/shard_map/ppermute | solution.py:163
  20.6 0.0 collective-permute-done.8
  20.6 0.0 collective-permute-start.3
  20.6 0.0 collective-permute-done.9
  20.6 0.2 copy.10
  20.8 0.2 reshape.42.refs_1_
  21.0 0.0 collective-permute-done
  21.0 0.6 %collective-permute-start.4 = (bf16[1024,128]{1,0:T(8,128)(2,1)S(1)}, bf16[1024,128]{1,0:T(8,128)(2,1)S(1)}, u32[]{:S(2)}, u32[]{:S(2)}) collective-permute-start(bf16[1024,128]{1,0:T(8,128)(2,1)S(1)} %collective-permute-done), channel_id=1, source_target_pairs={{0,1},{1,0},{2,3},{3,2},{4,5},{5,4},{6,7},{7,6},{8,9},{9,8},{10,11... | collective-permute-start | bytes 786440 | tf_op jit(solution)/shard_map/ppermute | solution.py:165
  21.6 2.1 %collective-permute-done.1 = bf16[1024,128]{1,0:T(8,128)(2,1)S(1)} collective-permute-done((bf16[1024,128]{1,0:T(8,128)(2,1)}, bf16[1024,128]{1,0:T(8,128)(2,1)S(1)}, u32[]{:S(2)}, u32[]{:S(2)}) %collective-permute-start.1) | collective-permute-done | bytes 262176 | tf_op jit(solution)/shard_map/ppermute | solution.py:163
  23.6 0.0 collective-permute-start.5
  23.7 5.5 %collective-permute-done.2 = bf16[1024,128]{1,0:T(8,128)(2,1)} collective-permute-done((bf16[1024,128]{1,0:T(8,128)(2,1)}, bf16[1024,128]{1,0:T(8,128)(2,1)}, u32[]{:S(2)}, u32[]{:S(2)}) %collective-permute-start.2) | collective-permute-done | bytes 262176 | tf_op jit(solution)/shard_map/ppermute | solution.py:163
  29.2 0.0 collective-permute-start.6
  29.3 1.0 %constant_dynamic-update-slice_fusion.4 = bf16[8192,128]{1,0:T(8,128)(2,1)S(1)} fusion(bf16[8192,128]{1,0:T(8,128)(2,1)S(1)} %constant_dynamic-update-slice_fusion.5, bf16[1024,128]{1,0:T(8,128)(2,1)} %collective-permute-done.2), kind=kLoop, calls=%fused_computation.24 | loop fusion | bytes 524288
  30.2 0.0 collective-permute-done.3
  30.2 1.0 %constant_dynamic-update-slice_fusion.3 = bf16[8192,128]{1,0:T(8,128)(2,1)S(1)} fusion(bf16[8192,128]{1,0:T(8,128)(2,1)S(1)} %constant_dynamic-update-slice_fusion.4, bf16[1024,128]{1,0:T(8,128)(2,1)} %collective-permute-done.3), kind=kLoop, calls=%fused_computation.23 | loop fusion | bytes 524288
  31.2 0.0 collective-permute-done.4
  31.3 0.0 collective-permute-done.5
  31.3 0.0 collective-permute-done.6
  31.4 5.1 %shard_map.60 = bf16[768,128]{1,0:T(8,128)(2,1)S(1)} custom-call(s32[1]{0:T(128)} %bitcast.2.refs_0_, bf16[768,128]{1,0:T(8,128)(2,1)S(1)} %reshape.42.refs_1_, bf16[8192,128]{1,0:T(8,128)(2,1)S(1)} %constant_dynamic-update-slice_fusion.refs_1_.refs_2_), custom_call_target="tpu_custom_call" | custom-call | flops 3221225472 | bytes 2490368 | tf_op jit(solution)/shard_map/pallas_call | solution.py:137
  36.5 0.1 reshape.43
  36.6 0.3 fusion.21
  36.9 2.5 %collective-permute-start.10 = (bf16[256,128]{1,0:T(8,128)(2,1)S(1)}, bf16[256,128]{1,0:T(8,128)(2,1)S(1)}, u32[]{:S(2)}, u32[]{:S(2)}) collective-permute-start(bf16[256,128]{1,0:T(8,128)(2,1)S(1)} %bitcast.29), channel_id=1, source_target_pairs={{0,24},{8,0},{16,8},{24,16},{1,25},{9,1},{17,9},{25,17},{2,26},{10... | collective-permute-start | bytes 196616 | tf_op jit(solution)/shard_map/ppermute | solution.py:154
  39.4 0.0 copy-start
  39.4 0.0 copy-start.1
  39.5 5.6 %collective-permute-start.11 = (bf16[256,128]{1,0:T(8,128)(2,1)S(1)}, bf16[256,128]{1,0:T(8,128)(2,1)S(1)}, u32[]{:S(2)}, u32[]{:S(2)}) collective-permute-start(bf16[256,128]{1,0:T(8,128)(2,1)S(1)} %bitcast.30), channel_id=1, source_target_pairs={{0,16},{8,24},{16,0},{24,8},{1,17},{9,25},{17,1},{25,9},{2,18},{10... | collective-permute-start | bytes 196616 | tf_op jit(solution)/shard_map/ppermute | solution.py:154
  45.0 0.1 collective-permute-start.12
  45.1 3.7 %shard_map.59 = bf16[256,128]{1,0:T(8,128)(2,1)S(1)} custom-call(bf16[256,128]{1,0:T(8,128)(2,1)S(1)} %get-tuple-element.4.refs_0_, bf16[8192,128]{1,0:T(8,128)(2,1)S(1)} %constant_dynamic-update-slice_fusion.refs_1_.refs_2_), custom_call_target="tpu_custom_call" | custom-call | flops 1073741824 | bytes 2228224 | tf_op jit(solution)/shard_map/pallas_call | solution.py:141
  48.8 0.0 collective-permute-done.10
  48.8 0.0 collective-permute-done.11
  48.9 1.4 %collective-permute-done.12 = bf16[256,128]{1,0:T(8,128)(2,1)S(1)} collective-permute-done((bf16[256,128]{1,0:T(8,128)(2,1)S(1)}, bf16[256,128]{1,0:T(8,128)(2,1)S(1)}, u32[]{:S(2)}, u32[]{:S(2)}) %collective-permute-start.12) | collective-permute-done | bytes 65568 | tf_op jit(solution)/shard_map/ppermute | solution.py:154
  50.3 0.0 copy-done
  50.3 0.0 copy-done.1
  50.3 1.2 %subtract_convert_fusion = (bf16[512,128]{1,0:T(8,128)(2,1)}, bf16[512,128]{1,0:T(8,128)(2,1)}) fusion(f32[512]{0:T(512)S(1)} %copy-done.1, bf16[512,128]{1,0:T(8,128)(2,1)S(1)} %copy-done, bf16[256,128]{1,0:T(8,128)(2,1)S(1)} %collective-permute-done.12, bf16[256,128]{1,0:T(8,128)(2,1)S(1)} %collective-permute-done.11, ...), kind=kOutput, calls=%fused_computation.12 | convolution fusion | flops 136314880 | bytes 659456 | tf_op jit(solution)/shard_map/dot_general | solution.py:192
  (10 shorter events, 0.3 us)
Async XLA Ops:
  0.6 20.3 %collective-permute-start = (bf16[1024,128]{1,0:T(8,128)(2,1)}, bf16[1024,128]{1,0:T(8,128)(2,1)S(1)}, u32[]{:S(2)}, u32[]{:S(2)}) collective-permute-start(bf16[1024,128]{1,0:T(8,128)(2,1)} %param.7), channel_id=1, source_target_pairs={{0,2},{1,3},{2,4},{3,5},{4,6},{5,7},{6,0},{7,1},{8,10},{9,11},{10,... | collective-permute-start | bytes 786440 | tf_op jit(solution)/shard_map/ppermute | solution.py:163
  3.7 19.9 %collective-permute-start.1 = (bf16[1024,128]{1,0:T(8,128)(2,1)}, bf16[1024,128]{1,0:T(8,128)(2,1)S(1)}, u32[]{:S(2)}, u32[]{:S(2)}) collective-permute-start(bf16[1024,128]{1,0:T(8,128)(2,1)} %param.7), channel_id=1, source_target_pairs={{0,4},{1,5},{2,6},{3,7},{4,0},{5,1},{6,2},{7,3},{8,12},{9,13},{10,... | collective-permute-start | bytes 786440 | tf_op jit(solution)/shard_map/ppermute | solution.py:163
  13.0 6.1 %collective-permute-start.7 = (bf16[256,128]{1,0:T(8,128)(2,1)S(1)}, bf16[256,128]{1,0:T(8,128)(2,1)S(1)}, u32[]{:S(2)}, u32[]{:S(2)}) collective-permute-start(bf16[256,128]{1,0:T(8,128)(2,1)S(1)} %get-tuple-element.7), channel_id=1, source_target_pairs={{0,8},{8,16},{16,24},{24,0},{1,9},{9,17},{17,25},{25,1},{2,10},{10... | collective-permute-start | bytes 196616 | tf_op jit(solution)/shard_map/ppermute | solution.py:154
  14.6 6.0 %collective-permute-start.8 = (bf16[256,128]{1,0:T(8,128)(2,1)S(1)}, bf16[256,128]{1,0:T(8,128)(2,1)S(1)}, u32[]{:S(2)}, u32[]{:S(2)}) collective-permute-start(bf16[256,128]{1,0:T(8,128)(2,1)S(1)} %get-tuple-element.6), channel_id=1, source_target_pairs={{0,16},{8,24},{16,0},{24,8},{1,17},{9,25},{17,1},{25,9},{2,18},{10... | collective-permute-start | bytes 196616 | tf_op jit(solution)/shard_map/ppermute | solution.py:154
  16.1 4.5 %collective-permute-start.9 = (bf16[256,128]{1,0:T(8,128)(2,1)S(1)}, bf16[256,128]{1,0:T(8,128)(2,1)S(1)}, u32[]{:S(2)}, u32[]{:S(2)}) collective-permute-start(bf16[256,128]{1,0:T(8,128)(2,1)S(1)} %get-tuple-element.5), channel_id=1, source_target_pairs={{0,24},{8,0},{16,8},{24,16},{1,25},{9,1},{17,9},{25,17},{2,26},{10... | collective-permute-start | bytes 196616 | tf_op jit(solution)/shard_map/ppermute | solution.py:154
  19.2 10.1 %collective-permute-start.2 = (bf16[1024,128]{1,0:T(8,128)(2,1)}, bf16[1024,128]{1,0:T(8,128)(2,1)}, u32[]{:S(2)}, u32[]{:S(2)}) collective-permute-start(bf16[1024,128]{1,0:T(8,128)(2,1)} %param.7), channel_id=1, source_target_pairs={{0,6},{1,7},{2,0},{3,1},{4,2},{5,3},{6,4},{7,5},{8,14},{9,15},{10,... | collective-permute-start | bytes 786440 | tf_op jit(solution)/shard_map/ppermute | solution.py:163
  20.6 9.7 %collective-permute-start.3 = (bf16[1024,128]{1,0:T(8,128)(2,1)}, bf16[1024,128]{1,0:T(8,128)(2,1)}, u32[]{:S(2)}, u32[]{:S(2)}) collective-permute-start(bf16[1024,128]{1,0:T(8,128)(2,1)} %param.7), channel_id=1, source_target_pairs={{0,1},{1,0},{2,3},{3,2},{4,5},{5,4},{6,7},{7,6},{8,9},{9,8},{10,11... | collective-permute-start | bytes 786440 | tf_op jit(solution)/shard_map/ppermute | solution.py:165
  21.0 10.3 %collective-permute-start.4 = (bf16[1024,128]{1,0:T(8,128)(2,1)S(1)}, bf16[1024,128]{1,0:T(8,128)(2,1)S(1)}, u32[]{:S(2)}, u32[]{:S(2)}) collective-permute-start(bf16[1024,128]{1,0:T(8,128)(2,1)S(1)} %collective-permute-done), channel_id=1, source_target_pairs={{0,1},{1,0},{2,3},{3,2},{4,5},{5,4},{6,7},{7,6},{8,9},{9,8},{10,11... | collective-permute-start | bytes 786440 | tf_op jit(solution)/shard_map/ppermute | solution.py:165
  23.6 7.6 %collective-permute-start.5 = (bf16[1024,128]{1,0:T(8,128)(2,1)S(1)}, bf16[1024,128]{1,0:T(8,128)(2,1)S(1)}, u32[]{:S(2)}, u32[]{:S(2)}) collective-permute-start(bf16[1024,128]{1,0:T(8,128)(2,1)S(1)} %collective-permute-done.1), channel_id=1, source_target_pairs={{0,1},{1,0},{2,3},{3,2},{4,5},{5,4},{6,7},{7,6},{8,9},{9,8},{10,11... | collective-permute-start | bytes 786440 | tf_op jit(solution)/shard_map/ppermute | solution.py:165
  29.2 2.1 %collective-permute-start.6 = (bf16[1024,128]{1,0:T(8,128)(2,1)}, bf16[1024,128]{1,0:T(8,128)(2,1)S(1)}, u32[]{:S(2)}, u32[]{:S(2)}) collective-permute-start(bf16[1024,128]{1,0:T(8,128)(2,1)} %collective-permute-done.2), channel_id=1, source_target_pairs={{0,1},{1,0},{2,3},{3,2},{4,5},{5,4},{6,7},{7,6},{8,9},{9,8},{10,11... | collective-permute-start | bytes 786440 | tf_op jit(solution)/shard_map/ppermute | solution.py:165
  36.9 11.9 %collective-permute-start.10 = (bf16[256,128]{1,0:T(8,128)(2,1)S(1)}, bf16[256,128]{1,0:T(8,128)(2,1)S(1)}, u32[]{:S(2)}, u32[]{:S(2)}) collective-permute-start(bf16[256,128]{1,0:T(8,128)(2,1)S(1)} %bitcast.29), channel_id=1, source_target_pairs={{0,24},{8,0},{16,8},{24,16},{1,25},{9,1},{17,9},{25,17},{2,26},{10... | collective-permute-start | bytes 196616 | tf_op jit(solution)/shard_map/ppermute | solution.py:154
  39.4 10.8 %copy-start = (bf16[512,128]{1,0:T(8,128)(2,1)S(1)}, bf16[512,128]{1,0:T(8,128)(2,1)}, u32[]{:S(2)}) copy-start(bf16[512,128]{1,0:T(8,128)(2,1)} %param.4) | copy-start | bytes 393220
  39.4 10.8 %copy-start.1 = (f32[512]{0:T(512)S(1)}, f32[512]{0:T(512)}, u32[]{:S(2)}) copy-start(f32[512]{0:T(512)} %param.5) | copy-start | bytes 6148
  39.5 9.4 %collective-permute-start.11 = (bf16[256,128]{1,0:T(8,128)(2,1)S(1)}, bf16[256,128]{1,0:T(8,128)(2,1)S(1)}, u32[]{:S(2)}, u32[]{:S(2)}) collective-permute-start(bf16[256,128]{1,0:T(8,128)(2,1)S(1)} %bitcast.30), channel_id=1, source_target_pairs={{0,16},{8,24},{16,0},{24,8},{1,17},{9,25},{17,1},{25,9},{2,18},{10... | collective-permute-start | bytes 196616 | tf_op jit(solution)/shard_map/ppermute | solution.py:154
  45.0 5.2 %collective-permute-start.12 = (bf16[256,128]{1,0:T(8,128)(2,1)S(1)}, bf16[256,128]{1,0:T(8,128)(2,1)S(1)}, u32[]{:S(2)}, u32[]{:S(2)}) collective-permute-start(bf16[256,128]{1,0:T(8,128)(2,1)S(1)} %bitcast.31), channel_id=1, source_target_pairs={{0,8},{8,16},{16,24},{24,0},{1,9},{9,17},{17,25},{25,1},{2,10},{10... | collective-permute-start | bytes 196616 | tf_op jit(solution)/shard_map/ppermute | solution.py:154

commit v4 on v3

--- a/solution.py
+++ b/solution.py
@@ -183,7 +183,15 @@
     real = jnp.sum((coarse_ids == me).astype(jnp.int32))
     remote = jnp.stack(arrived[1:], axis=1).reshape((loops - 1) * cap, width)
     count = ((loops - 1) * real).reshape(1)
-    first = soft_part(remote, part, final=True, count=count, tiles=2)
+    half = remote.shape[0] // 2
+    first = lax.cond(
+        count[0] > half,
+        lambda q, c, n: soft_part(q, c, final=True),
+        lambda q, c, n: soft_part(q, c, final=True, count=n, tiles=2),
+        remote,
+        part,
+        count,
+    )
     first = first.reshape(cap, loops - 1, width)
     ret = {d: _shift(first[:, d - 1], "cell", loops, -d) for d in range(1, loops)}
     ret[0] = soft_part(arrived[0], part, final=True)

time: 51.8 us -> 54 us (1.042)
  waiting for transfers between devices: 9.06 us -> 5.5 us
  local copies, waits for them, and re-layouts: 4.1 us -> 7.64 us
  Pallas kernels: 8.81 us -> 12 us
  starting transfers between devices: 20.3 us -> 19.5 us
    unnamed x14, local copies, waits for them, and re-layouts: 3.13 us -> 5.99 us
    ppermute x3, waiting for transfers between devices: 7.63 us -> 5.48 us  [_gather_partition(): pieces.append(lax.ppermute(centroids, 'blk', pairs))]
    pallas_call x1, Pallas kernels: 3.71 us -> 5.29 us  [soft_part(): pl.pallas_call(kernel, out_shape=out_shape, grid=(slots // tq,), in_specs...]
    pallas_call x1, Pallas kernels: 5.1 us -> 6.66 us  [soft_part(): pl.pallas_call(kernel, out_shape=out_shape, grid_spec=grid_spec, compiler...]
    ppermute x6, waiting for transfers between devices: 1.43 us -> 0.02 us  [_shift(): return lax.ppermute(x, axis, [(i, (i + d) % n) for i in range(n)])]
    ppermute x6, starting transfers between devices: 12.6 us -> 11.8 us  [_shift(): return lax.ppermute(x, axis, [(i, (i + d) % n) for i in range(n)])]
    concatenate x1, local copies, waits for them, and re-layouts: 0.04 us -> 0.71 us  [_gather_partition(): return jnp.concatenate(pieces + swapped, axis=0)]
  transfers between devices with their start and end apart: 13 -> 13, of which waited for: 3 -> 2; matrix products, arithmetic and copies ran while one was open for 20% -> 24% of each run, Pallas kernels for 7% -> 10%
where the time goes in v4:
time: 54 us; the launch traced here: 53.7 us
  starting transfers between devices  19.5 us (36%)
  Pallas kernels  12 us (22%)
  local copies, waits for them, and re-layouts  7.64 us (14%)
  other arithmetic  6.49 us (12%)
  waiting for transfers between devices  5.5 us (10%)
  between operations  1.46 us (3%)
  matrix products  1.22 us (2%)
    ppermute x6, starting transfers between devices, _shift(): return lax.ppermute(x, axis, [(i, (i + d) % n) for i in range(n)])  11.8 us
    ppermute x3, starting transfers between devices, _gather_partition(): pieces.append(lax.ppermute(centroids, 'blk', pairs))  7.1 us
    pallas_call x1, Pallas kernels, soft_part(): pl.pallas_call(kernel, out_shape=out_shape, grid_spec=grid_spec, compiler...  6.66 us
    unnamed x14, local copies, waits for them, and re-layouts  5.99 us
    ppermute x3, waiting for transfers between devices, _gather_partition(): pieces.append(lax.ppermute(centroids, 'blk', pairs))  5.48 us
    pallas_call x1, Pallas kernels, soft_part(): pl.pallas_call(kernel, out_shape=out_shape, grid=(slots // tq,), in_specs...  5.29 us
    scatter x1, other arithmetic, _local(): jnp.zeros((loops * cap, width), jnp.bfloat16).at[slots].set(dequant)  2.28 us
    another operation x2, other arithmetic  1.39 us
  transfers between devices with their start and end apart: 13, of which 2 were waited for; matrix products, arithmetic and copies ran while one was open for 24% of the time, Pallas kernels for 10%

profile of v4, /device:TPU:0, one launch (start us, length us, event | category | flops | bytes accessed | tf_op | source)
XLA Modules:
  0.0 53.7 jit_solution(6175620299691156776)
XLA Ops:
  0.6 3.1 %collective-permute-start = (bf16[1024,128]{1,0:T(8,128)(2,1)}, bf16[1024,128]{1,0:T(8,128)(2,1)S(1)}, u32[]{:S(2)}, u32[]{:S(2)}) collective-permute-start(bf16[1024,128]{1,0:T(8,128)(2,1)} %param.9), channel_id=1, source_target_pairs={{0,2},{1,3},{2,4},{3,5},{4,6},{5,7},{6,0},{7,1},{8,10},{9,11},{10,... | collective-permute-start | bytes 786440 | tf_op jit(solution)/shard_map/ppermute | solution.py:163
  3.7 2.6 %collective-permute-start.1 = (bf16[1024,128]{1,0:T(8,128)(2,1)}, bf16[1024,128]{1,0:T(8,128)(2,1)S(1)}, u32[]{:S(2)}, u32[]{:S(2)}) collective-permute-start(bf16[1024,128]{1,0:T(8,128)(2,1)} %param.9), channel_id=1, source_target_pairs={{0,4},{1,5},{2,6},{3,7},{4,0},{5,1},{6,2},{7,3},{8,12},{9,13},{10,... | collective-permute-start | bytes 786440 | tf_op jit(solution)/shard_map/ppermute | solution.py:163
  6.3 0.7 %fusion.14 = s32[4,4,128]{2,1,0:T(4,128)S(1)} fusion(s32[4,128]{1,0:T(4,128)} %bitcast.35), kind=kLoop, calls=%fused_computation.35 | loop fusion | flops 4096 | bytes 10240 | tf_op jit(solution)/shard_map/convert_element_type | solution.py:176
  7.0 1.2 %reduce-window.6 = s32[4,4,128]{2,1,0:T(4,128)S(1)} reduce-window(s32[4,4,128]{2,1,0:T(4,128)S(1)} %fusion.14, s32[]{:T(128)} %constant.30.clone.1), window={size=1x1x128 pad=0_0x0_0x127_0}, to_apply=%region_0.0 | reduce-window | flops 260096 | bytes 16388 | tf_op jit(solution)/shard_map/reduce-window
  8.2 0.2 slice_reduce_fusion
  8.4 0.2 reduce-window.9
  8.6 0.1 add_bitcast_fusion
  8.7 0.7 %fusion.13 = s32[512]{0:T(512)S(1)} fusion(s32[1,4,4,128]{3,2,1,0:T(4,128)S(1)} %add_bitcast_fusion, s32[512]{0:T(512)} %param.8), kind=kLoop, calls=%fused_computation.30 | loop fusion | flops 5632 | bytes 12288 | tf_op jit(solution)/shard_map/reduce_sum | solution.py:177
  9.4 1.3 %compare_select_fusion = (s32[512]{0:T(512)S(1)}, s32[512]{0:T(512)S(1)}, s32[]{:T(128)}) fusion(s32[512]{0:T(512)S(1)} %fusion.13, s32[512]{0:T(512)} %param.8, s32[]{:T(128)S(6)} %axis_index.15), kind=kLoop, calls=%fused_computation.36 | loop fusion | flops 10751 | bytes 8200 | tf_op jit(solution)/shard_map/select_n | solution.py:179
  10.7 2.3 %scatter_custom_fusion = bf16[1024,128]{1,0:T(8,128)(2,1)S(1)} fusion(s32[512]{0:T(512)S(1)} %get-tuple-element.21, bf16[]{:T(256)} %constant.35.clone.1, bf16[512,128]{1,0:T(8,128)(2,1)} %param.6, f32[512]{0:T(512)} %param.7), kind=kCustom, calls=%fused_computation.15 | custom fusion | flops 196608 | bytes 395266 | tf_op jit(solution)/shard_map/scatter | solution.py:179
  13.0 1.5 %collective-permute-start.7 = (bf16[256,128]{1,0:T(8,128)(2,1)S(1)}, bf16[256,128]{1,0:T(8,128)(2,1)S(1)}, u32[]{:S(2)}, u32[]{:S(2)}) collective-permute-start(bf16[256,128]{1,0:T(8,128)(2,1)S(1)} %get-tuple-element.26), channel_id=1, source_target_pairs={{0,8},{8,16},{16,24},{24,0},{1,9},{9,17},{17,25},{25,1},{2,10},{10... | collective-permute-start | bytes 196616 | tf_op jit(solution)/shard_map/ppermute | solution.py:154
  14.6 1.5 %collective-permute-start.8 = (bf16[256,128]{1,0:T(8,128)(2,1)S(1)}, bf16[256,128]{1,0:T(8,128)(2,1)S(1)}, u32[]{:S(2)}, u32[]{:S(2)}) collective-permute-start(bf16[256,128]{1,0:T(8,128)(2,1)S(1)} %get-tuple-element.25), channel_id=1, source_target_pairs={{0,16},{8,24},{16,0},{24,8},{1,17},{9,25},{17,1},{25,9},{2,18},{10... | collective-permute-start | bytes 196616 | tf_op jit(solution)/shard_map/ppermute | solution.py:154
  16.1 1.4 %collective-permute-start.9 = (bf16[256,128]{1,0:T(8,128)(2,1)S(1)}, bf16[256,128]{1,0:T(8,128)(2,1)S(1)}, u32[]{:S(2)}, u32[]{:S(2)}) collective-permute-start(bf16[256,128]{1,0:T(8,128)(2,1)S(1)} %get-tuple-element.24), channel_id=1, source_target_pairs={{0,24},{8,0},{16,8},{24,16},{1,25},{9,1},{17,9},{25,17},{2,26},{10... | collective-permute-start | bytes 196616 | tf_op jit(solution)/shard_map/ppermute | solution.py:154
  17.5 1.7 %constant_dynamic-update-slice_fusion.7 = bf16[8192,128]{1,0:T(8,128)(2,1)} fusion(bf16[1024,128]{1,0:T(8,128)(2,1)} %param.9), kind=kLoop, calls=%fused_computation.27 | loop fusion | bytes 524288
  19.9 0.0 collective-permute-done.7
  19.9 1.4 %collective-permute-start.2 = (bf16[1024,128]{1,0:T(8,128)(2,1)}, bf16[1024,128]{1,0:T(8,128)(2,1)S(1)}, u32[]{:S(2)}, u32[]{:S(2)}) collective-permute-start(bf16[1024,128]{1,0:T(8,128)(2,1)} %param.9), channel_id=1, source_target_pairs={{0,6},{1,7},{2,0},{3,1},{4,2},{5,3},{6,4},{7,5},{8,14},{9,15},{10,... | collective-permute-start | bytes 786440 | tf_op jit(solution)/shard_map/ppermute | solution.py:163
  21.3 0.0 collective-permute-done.8
  21.3 0.0 collective-permute-start.3
  21.3 0.0 collective-permute-done.9
  21.3 0.2 copy.6
  21.5 0.2 reshape.42
  21.7 0.0 collective-permute-done
  21.7 0.6 %collective-permute-start.4 = (bf16[1024,128]{1,0:T(8,128)(2,1)S(1)}, bf16[1024,128]{1,0:T(8,128)(2,1)S(1)}, u32[]{:S(2)}, u32[]{:S(2)}) collective-permute-start(bf16[1024,128]{1,0:T(8,128)(2,1)S(1)} %collective-permute-done), channel_id=1, source_target_pairs={{0,1},{1,0},{2,3},{3,2},{4,5},{5,4},{6,7},{7,6},{8,9},{9,8},{10,11... | collective-permute-start | bytes 786440 | tf_op jit(solution)/shard_map/ppermute | solution.py:165
  22.2 0.7 %constant_dynamic-update-slice_fusion.6 = bf16[8192,128]{1,0:T(8,128)(2,1)} fusion(bf16[8192,128]{1,0:T(8,128)(2,1)} %constant_dynamic-update-slice_fusion.7, bf16[1024,128]{1,0:T(8,128)(2,1)S(1)} %collective-permute-done), kind=kLoop, calls=%fused_computation.26 | loop fusion | bytes 524288
  22.9 0.7 %collective-permute-done.1 = bf16[1024,128]{1,0:T(8,128)(2,1)S(1)} collective-permute-done((bf16[1024,128]{1,0:T(8,128)(2,1)}, bf16[1024,128]{1,0:T(8,128)(2,1)S(1)}, u32[]{:S(2)}, u32[]{:S(2)}) %collective-permute-start.1) | collective-permute-done | bytes 262176 | tf_op jit(solution)/shard_map/ppermute | solution.py:163
  23.6 0.0 collective-permute-start.5
  23.7 0.7 %constant_dynamic-update-slice_fusion.5 = bf16[8192,128]{1,0:T(8,128)(2,1)} fusion(bf16[8192,128]{1,0:T(8,128)(2,1)} %constant_dynamic-update-slice_fusion.6, bf16[1024,128]{1,0:T(8,128)(2,1)S(1)} %collective-permute-done.1), kind=kLoop, calls=%fused_computation.25 | loop fusion | bytes 524288
  24.4 4.8 %collective-permute-done.2 = bf16[1024,128]{1,0:T(8,128)(2,1)S(1)} collective-permute-done((bf16[1024,128]{1,0:T(8,128)(2,1)}, bf16[1024,128]{1,0:T(8,128)(2,1)S(1)}, u32[]{:S(2)}, u32[]{:S(2)}) %collective-permute-start.2) | collective-permute-done | bytes 262176 | tf_op jit(solution)/shard_map/ppermute | solution.py:163
  29.1 0.0 collective-permute-start.6
  29.1 0.7 %constant_dynamic-update-slice_fusion.4 = bf16[8192,128]{1,0:T(8,128)(2,1)} fusion(bf16[8192,128]{1,0:T(8,128)(2,1)} %constant_dynamic-update-slice_fusion.5, bf16[1024,128]{1,0:T(8,128)(2,1)S(1)} %collective-permute-done.2), kind=kLoop, calls=%fused_computation.24 | loop fusion | bytes 524288
  29.9 0.0 collective-permute-done.3
  29.9 0.7 %constant_dynamic-update-slice_fusion.3 = bf16[8192,128]{1,0:T(8,128)(2,1)} fusion(bf16[8192,128]{1,0:T(8,128)(2,1)} %constant_dynamic-update-slice_fusion.4, bf16[1024,128]{1,0:T(8,128)(2,1)S(1)} %collective-permute-done.3), kind=kLoop, calls=%fused_computation.23 | loop fusion | bytes 524288
  30.6 0.0 collective-permute-done.4
  30.6 0.7 %constant_dynamic-update-slice_fusion.2 = bf16[8192,128]{1,0:T(8,128)(2,1)} fusion(bf16[8192,128]{1,0:T(8,128)(2,1)} %constant_dynamic-update-slice_fusion.3, bf16[1024,128]{1,0:T(8,128)(2,1)S(1)} %collective-permute-done.4), kind=kLoop, calls=%fused_computation.22 | loop fusion | bytes 524288
  31.3 0.0 collective-permute-done.5
  31.3 0.7 %constant_dynamic-update-slice_fusion.1 = bf16[8192,128]{1,0:T(8,128)(2,1)} fusion(bf16[8192,128]{1,0:T(8,128)(2,1)} %constant_dynamic-update-slice_fusion.2, bf16[1024,128]{1,0:T(8,128)(2,1)S(1)} %collective-permute-done.5), kind=kLoop, calls=%fused_computation.21 | loop fusion | bytes 524288
  32.0 0.0 collective-permute-done.6
  32.0 0.7 %constant_dynamic-update-slice_fusion.refs_1_ = bf16[8192,128]{1,0:T(8,128)(2,1)} fusion(bf16[8192,128]{1,0:T(8,128)(2,1)} %constant_dynamic-update-slice_fusion.1, bf16[1024,128]{1,0:T(8,128)(2,1)S(1)} %collective-permute-done.6), kind=kLoop, calls=%fused_computation.20 | loop fusion | bytes 524288 | tf_op jit(solution)/shard_map/concatenate | solution.py:166
  32.7 6.7 %conditional.1 = (bf16[768,128]{1,0:T(8,128)(2,1)S(1)}) conditional(s32[]{:T(128)} %convert_element_type.34, (s32[]{:T(128)}, bf16[768,128]{1,0:T(8,128)(2,1)S(1)}, bf16[8192,128]{1,0:T(8,128)(2,1)}) %tuple.14, (bf16[768,128]{1,0:T(8,128)(2,1)S(1)}, bf16[8192,128]{1,0:T(8,128)(2,1)}) %tuple.15), branch_computations={%region_5.6_spmd, %region_6.7_spmd} | conditional | flops 3221225472 | bytes 2490376 | solution.py:187
  32.7 6.7 %branch_0_fun.1 = bf16[768,128]{1,0:T(8,128)(2,1)S(1)} custom-call(s32[1]{0:T(128)} %bitcast.refs_0_, bf16[768,128]{1,0:T(8,128)(2,1)S(1)} %get-tuple-element.15.refs_1_, bf16[8192,128]{1,0:T(8,128)(2,1)} %get-tuple-element.16.refs_2_), custom_call_target="tpu_custom_call" | custom-call | flops 3221225472 | bytes 2490368 | tf_op jit(solution)/shard_map/cond/branch_0_fun/pallas_call | solution.py:137
  39.4 0.1 reshape.43
  39.5 0.3 fusion.21
  39.8 2.5 %collective-permute-start.10 = (bf16[256,128]{1,0:T(8,128)(2,1)S(1)}, bf16[256,128]{1,0:T(8,128)(2,1)S(1)}, u32[]{:S(2)}, u32[]{:S(2)}) collective-permute-start(bf16[256,128]{1,0:T(8,128)(2,1)S(1)} %bitcast.29), channel_id=1, source_target_pairs={{0,24},{8,0},{16,8},{24,16},{1,25},{9,1},{17,9},{25,17},{2,26},{10... | collective-permute-start | bytes 196616 | tf_op jit(solution)/shard_map/ppermute | solution.py:154
  42.3 0.0 copy-start
  42.4 0.0 copy-start.1
  42.4 4.7 %collective-permute-start.11 = (bf16[256,128]{1,0:T(8,128)(2,1)S(1)}, bf16[256,128]{1,0:T(8,128)(2,1)S(1)}, u32[]{:S(2)}, u32[]{:S(2)}) collective-permute-start(bf16[256,128]{1,0:T(8,128)(2,1)S(1)} %bitcast.30), channel_id=1, source_target_pairs={{0,16},{8,24},{16,0},{24,8},{1,17},{9,25},{17,1},{25,9},{2,18},{10... | collective-permute-start | bytes 196616 | tf_op jit(solution)/shard_map/ppermute | solution.py:154
  47.1 0.1 collective-permute-start.12
  47.2 5.3 %shard_map.59 = bf16[256,128]{1,0:T(8,128)(2,1)S(1)} custom-call(bf16[256,128]{1,0:T(8,128)(2,1)S(1)} %get-tuple-element.23.refs_0_, bf16[8192,128]{1,0:T(8,128)(2,1)} %constant_dynamic-update-slice_fusion.refs_1_), custom_call_target="tpu_custom_call" | custom-call | flops 1073741824 | bytes 2228224 | tf_op jit(solution)/shard_map/pallas_call | solution.py:141
  52.5 0.0 collective-permute-done.10
  52.5 0.0 collective-permute-done.11
  52.5 0.0 collective-permute-done.12
  52.5 0.0 copy-done
  52.5 0.0 copy-done.1
  52.5 1.2 %subtract_convert_fusion = (bf16[512,128]{1,0:T(8,128)(2,1)}, bf16[512,128]{1,0:T(8,128)(2,1)}) fusion(f32[512]{0:T(512)S(1)} %copy-done.1, bf16[512,128]{1,0:T(8,128)(2,1)S(1)} %copy-done, bf16[256,128]{1,0:T(8,128)(2,1)S(1)} %collective-permute-done.12, bf16[256,128]{1,0:T(8,128)(2,1)S(1)} %collective-permute-done.11, ...), kind=kOutput, calls=%fused_computation.12 | convolution fusion | flops 136314880 | bytes 659456 | tf_op jit(solution)/shard_map/dot_general | solution.py:200
  (5 shorter events, 0.1 us)
Async XLA Ops:
  0.6 21.0 %collective-permute-start = (bf16[1024,128]{1,0:T(8,128)(2,1)}, bf16[1024,128]{1,0:T(8,128)(2,1)S(1)}, u32[]{:S(2)}, u32[]{:S(2)}) collective-permute-start(bf16[1024,128]{1,0:T(8,128)(2,1)} %param.9), channel_id=1, source_target_pairs={{0,2},{1,3},{2,4},{3,5},{4,6},{5,7},{6,0},{7,1},{8,10},{9,11},{10,... | collective-permute-start | bytes 786440 | tf_op jit(solution)/shard_map/ppermute | solution.py:163
  3.7 19.9 %collective-permute-start.1 = (bf16[1024,128]{1,0:T(8,128)(2,1)}, bf16[1024,128]{1,0:T(8,128)(2,1)S(1)}, u32[]{:S(2)}, u32[]{:S(2)}) collective-permute-start(bf16[1024,128]{1,0:T(8,128)(2,1)} %param.9), channel_id=1, source_target_pairs={{0,4},{1,5},{2,6},{3,7},{4,0},{5,1},{6,2},{7,3},{8,12},{9,13},{10,... | collective-permute-start | bytes 786440 | tf_op jit(solution)/shard_map/ppermute | solution.py:163
  13.0 6.8 %collective-permute-start.7 = (bf16[256,128]{1,0:T(8,128)(2,1)S(1)}, bf16[256,128]{1,0:T(8,128)(2,1)S(1)}, u32[]{:S(2)}, u32[]{:S(2)}) collective-permute-start(bf16[256,128]{1,0:T(8,128)(2,1)S(1)} %get-tuple-element.26), channel_id=1, source_target_pairs={{0,8},{8,16},{16,24},{24,0},{1,9},{9,17},{17,25},{25,1},{2,10},{10... | collective-permute-start | bytes 196616 | tf_op jit(solution)/shard_map/ppermute | solution.py:154
  14.6 6.7 %collective-permute-start.8 = (bf16[256,128]{1,0:T(8,128)(2,1)S(1)}, bf16[256,128]{1,0:T(8,128)(2,1)S(1)}, u32[]{:S(2)}, u32[]{:S(2)}) collective-permute-start(bf16[256,128]{1,0:T(8,128)(2,1)S(1)} %get-tuple-element.25), channel_id=1, source_target_pairs={{0,16},{8,24},{16,0},{24,8},{1,17},{9,25},{17,1},{25,9},{2,18},{10... | collective-permute-start | bytes 196616 | tf_op jit(solution)/shard_map/ppermute | solution.py:154
  16.1 5.2 %collective-permute-start.9 = (bf16[256,128]{1,0:T(8,128)(2,1)S(1)}, bf16[256,128]{1,0:T(8,128)(2,1)S(1)}, u32[]{:S(2)}, u32[]{:S(2)}) collective-permute-start(bf16[256,128]{1,0:T(8,128)(2,1)S(1)} %get-tuple-element.24), channel_id=1, source_target_pairs={{0,24},{8,0},{16,8},{24,16},{1,25},{9,1},{17,9},{25,17},{2,26},{10... | collective-permute-start | bytes 196616 | tf_op jit(solution)/shard_map/ppermute | solution.py:154
  19.9 9.3 %collective-permute-start.2 = (bf16[1024,128]{1,0:T(8,128)(2,1)}, bf16[1024,128]{1,0:T(8,128)(2,1)S(1)}, u32[]{:S(2)}, u32[]{:S(2)}) collective-permute-start(bf16[1024,128]{1,0:T(8,128)(2,1)} %param.9), channel_id=1, source_target_pairs={{0,6},{1,7},{2,0},{3,1},{4,2},{5,3},{6,4},{7,5},{8,14},{9,15},{10,... | collective-permute-start | bytes 786440 | tf_op jit(solution)/shard_map/ppermute | solution.py:163
  21.3 8.6 %collective-permute-start.3 = (bf16[1024,128]{1,0:T(8,128)(2,1)}, bf16[1024,128]{1,0:T(8,128)(2,1)S(1)}, u32[]{:S(2)}, u32[]{:S(2)}) collective-permute-start(bf16[1024,128]{1,0:T(8,128)(2,1)} %param.9), channel_id=1, source_target_pairs={{0,1},{1,0},{2,3},{3,2},{4,5},{5,4},{6,7},{7,6},{8,9},{9,8},{10,11... | collective-permute-start | bytes 786440 | tf_op jit(solution)/shard_map/ppermute | solution.py:165
  21.7 8.9 %collective-permute-start.4 = (bf16[1024,128]{1,0:T(8,128)(2,1)S(1)}, bf16[1024,128]{1,0:T(8,128)(2,1)S(1)}, u32[]{:S(2)}, u32[]{:S(2)}) collective-permute-start(bf16[1024,128]{1,0:T(8,128)(2,1)S(1)} %collective-permute-done), channel_id=1, source_target_pairs={{0,1},{1,0},{2,3},{3,2},{4,5},{5,4},{6,7},{7,6},{8,9},{9,8},{10,11... | collective-permute-start | bytes 786440 | tf_op jit(solution)/shard_map/ppermute | solution.py:165
  23.6 7.6 %collective-permute-start.5 = (bf16[1024,128]{1,0:T(8,128)(2,1)S(1)}, bf16[1024,128]{1,0:T(8,128)(2,1)S(1)}, u32[]{:S(2)}, u32[]{:S(2)}) collective-permute-start(bf16[1024,128]{1,0:T(8,128)(2,1)S(1)} %collective-permute-done.1), channel_id=1, source_target_pairs={{0,1},{1,0},{2,3},{3,2},{4,5},{5,4},{6,7},{7,6},{8,9},{9,8},{10,11... | collective-permute-start | bytes 786440 | tf_op jit(solution)/shard_map/ppermute | solution.py:165
  29.1 2.9 %collective-permute-start.6 = (bf16[1024,128]{1,0:T(8,128)(2,1)S(1)}, bf16[1024,128]{1,0:T(8,128)(2,1)S(1)}, u32[]{:S(2)}, u32[]{:S(2)}) collective-permute-start(bf16[1024,128]{1,0:T(8,128)(2,1)S(1)} %collective-permute-done.2), channel_id=1, source_target_pairs={{0,1},{1,0},{2,3},{3,2},{4,5},{5,4},{6,7},{7,6},{8,9},{9,8},{10,11... | collective-permute-start | bytes 786440 | tf_op jit(solution)/shard_map/ppermute | solution.py:165
  39.8 12.7 %collective-permute-start.10 = (bf16[256,128]{1,0:T(8,128)(2,1)S(1)}, bf16[256,128]{1,0:T(8,128)(2,1)S(1)}, u32[]{:S(2)}, u32[]{:S(2)}) collective-permute-start(bf16[256,128]{1,0:T(8,128)(2,1)S(1)} %bitcast.29), channel_id=1, source_target_pairs={{0,24},{8,0},{16,8},{24,16},{1,25},{9,1},{17,9},{25,17},{2,26},{10... | collective-permute-start | bytes 196616 | tf_op jit(solution)/shard_map/ppermute | solution.py:154
  42.3 10.2 %copy-start = (bf16[512,128]{1,0:T(8,128)(2,1)S(1)}, bf16[512,128]{1,0:T(8,128)(2,1)}, u32[]{:S(2)}) copy-start(bf16[512,128]{1,0:T(8,128)(2,1)} %param.6) | copy-start | bytes 393220
  42.4 10.2 %copy-start.1 = (f32[512]{0:T(512)S(1)}, f32[512]{0:T(512)}, u32[]{:S(2)}) copy-start(f32[512]{0:T(512)} %param.7) | copy-start | bytes 6148
  42.4 10.1 %collective-permute-start.11 = (bf16[256,128]{1,0:T(8,128)(2,1)S(1)}, bf16[256,128]{1,0:T(8,128)(2,1)S(1)}, u32[]{:S(2)}, u32[]{:S(2)}) collective-permute-start(bf16[256,128]{1,0:T(8,128)(2,1)S(1)} %bitcast.30), channel_id=1, source_target_pairs={{0,16},{8,24},{16,0},{24,8},{1,17},{9,25},{17,1},{25,9},{2,18},{10... | collective-permute-start | bytes 196616 | tf_op jit(solution)/shard_map/ppermute | solution.py:154
  47.1 5.4 %collective-permute-start.12 = (bf16[256,128]{1,0:T(8,128)(2,1)S(1)}, bf16[256,128]{1,0:T(8,128)(2,1)S(1)}, u32[]{:S(2)}, u32[]{:S(2)}) collective-permute-start(bf16[256,128]{1,0:T(8,128)(2,1)S(1)} %bitcast.31), channel_id=1, source_target_pairs={{0,8},{8,16},{16,24},{24,0},{1,9},{9,17},{17,25},{25,1},{2,10},{10... | collective-permute-start | bytes 196616 | tf_op jit(solution)/shard_map/ppermute | solution.py:154

commit v5 on v0

--- a/solution.py
+++ b/solution.py
@@ -124,7 +124,7 @@
     n_blk = lax.axis_size("blk")
     n_chip = n_blk // 2
     pieces = [centroids]
-    for d in range(1, n_chip):
+    for d in sorted(range(1, n_chip), key=lambda d: -min(d, n_chip - d) * 10 - d):
         pairs = [(k * 2 + c, ((k + d) % n_chip) * 2 + c) for k in range(n_chip) for c in range(2)]
         pieces.append(lax.ppermute(centroids, "blk", pairs))
     swap = [(b, b ^ 1) for b in range(n_blk)]
@@ -149,7 +149,10 @@
     first = soft_part(jnp.concatenate(arrived[1:], axis=0), part, final=True)
     ret = {d: _shift(first[(d - 1) * cap:d * cap], "cell", loops, -d) for d in range(1, loops)}
     ret[0] = soft_part(arrived[0], part, final=True)
-    mine = jnp.concatenate([ret[d] for d in range(loops)], axis=0)[slots]
+    back = jnp.concatenate([ret[d] for d in range(loops)], axis=0)
+    pick = slots[:, None] == jnp.arange(back.shape[0], dtype=jnp.int32)[None, :]
+    mine = jnp.dot(pick.astype(jnp.bfloat16), back, preferred_element_type=jnp.float32)
+    mine = mine.astype(jnp.bfloat16)
     residual = (dequant.astype(jnp.float32) - mine.astype(jnp.float32)).astype(jnp.bfloat16)
     return (mine, residual)
 

time: 50.6 us -> 47.3 us (0.935)
  the two profiles are of different devices: /device:TPU:0 before, /device:TPU:18 now
where the time goes in v5:
time: 47.3 us; the launch traced here: 47.1 us
  waiting for transfers between devices  13.4 us (28%)
  Pallas kernels  12.9 us (27%)
  starting transfers between devices  11.4 us (24%)
  other arithmetic  5.85 us (12%)
  local copies, waits for them, and re-layouts  1.48 us (3%)
  matrix products  1.22 us (3%)
  between operations  0.84 us (2%)
    pallas_call x2, Pallas kernels, soft_part(): pl.pallas_call(functools.partial(_soft_kernel, chunk=chunk, beta=1.0 / ma...  12.9 us
    ppermute x3, waiting for transfers between devices, _gather_partition(): pieces.append(lax.ppermute(centroids, 'blk', pairs))  9.51 us
    ppermute x6, starting transfers between devices, _shift(): return lax.ppermute(x, axis, [(i, (i + d) % n) for i in range(n)])  8.1 us
    ppermute x3, starting transfers between devices, _gather_partition(): pieces.append(lax.ppermute(centroids, 'blk', pairs))  3.16 us
    ppermute x6, waiting for transfers between devices, _shift(): return lax.ppermute(x, axis, [(i, (i + d) % n) for i in range(n)])  2.57 us
    scatter x1, other arithmetic, _local(): jnp.zeros((loops * cap, width), jnp.bfloat16).at[slots].set(dequant)  2.28 us
    another operation x2, other arithmetic  1.39 us
    ppermute x4, waiting for transfers between devices, _gather_partition(): swapped = [lax.ppermute(p, 'blk', swap) for p in pieces]  1.32 us
  transfers between devices with their start and end apart: 13, of which 5 were waited for; matrix products, arithmetic and copies ran while one was open for 15% of the time, Pallas kernels for 8%

profile of v5, /device:TPU:18, one launch (start us, length us, event | category | flops | bytes accessed | tf_op | source)
XLA Modules:
  0.0 47.1 jit_solution(6611826121220276646)
XLA Ops:
  0.6 0.4 collective-permute-start
  1.0 2.7 %collective-permute-start.1 = (bf16[1024,128]{1,0:T(8,128)(2,1)}, bf16[1024,128]{1,0:T(8,128)(2,1)S(1)}, u32[]{:S(2)}, u32[]{:S(2)}) collective-permute-start(bf16[1024,128]{1,0:T(8,128)(2,1)} %param.7), channel_id=1, source_target_pairs={{0,6},{1,7},{2,0},{3,1},{4,2},{5,3},{6,4},{7,5},{8,14},{9,15},{10,... | collective-permute-start | bytes 786440 | tf_op jit(solution)/shard_map/ppermute | solution.py:129
  3.7 0.7 %fusion.14 = s32[4,4,128]{2,1,0:T(4,128)S(1)} fusion(s32[4,128]{1,0:T(4,128)} %bitcast.16), kind=kLoop, calls=%fused_computation.32 | loop fusion | flops 4096 | bytes 10240 | tf_op jit(solution)/shard_map/convert_element_type | solution.py:142
  4.4 1.2 %reduce-window.6 = s32[4,4,128]{2,1,0:T(4,128)S(1)} reduce-window(s32[4,4,128]{2,1,0:T(4,128)S(1)} %fusion.14, s32[]{:T(128)} %constant.28.clone.1), window={size=1x1x128 pad=0_0x0_0x127_0}, to_apply=%region_0.0 | reduce-window | flops 260096 | bytes 16388 | tf_op jit(solution)/shard_map/reduce-window
  5.6 0.2 slice_reduce_fusion
  5.8 0.2 reduce-window.9
  6.0 0.1 add_bitcast_fusion
  6.1 0.7 %fusion.13 = s32[512]{0:T(512)S(1)} fusion(s32[1,4,4,128]{3,2,1,0:T(4,128)S(1)} %add_bitcast_fusion, s32[512]{0:T(512)} %param.6), kind=kLoop, calls=%fused_computation.27 | loop fusion | flops 5632 | bytes 12288 | tf_op jit(solution)/shard_map/reduce_sum | solution.py:143
  6.8 0.7 %compare_select_fusion = (s32[512]{0:T(512)S(1)}, s32[512]{0:T(512)S(1)}) fusion(s32[512]{0:T(512)S(1)} %fusion.13, s32[512]{0:T(512)} %param.6, s32[]{:T(128)S(6)} %axis_index.15), kind=kLoop, calls=%fused_computation.33 | loop fusion | flops 9216 | bytes 8196 | tf_op jit(solution)/shard_map/select_n | solution.py:145
  7.5 2.3 %scatter_custom_fusion = bf16[1024,128]{1,0:T(8,128)(2,1)S(1)} fusion(s32[512]{0:T(512)S(1)} %get-tuple-element.2, bf16[]{:T(256)} %constant.33.clone.1, bf16[512,128]{1,0:T(8,128)(2,1)} %param.4, f32[512]{0:T(512)} %param.5), kind=kCustom, calls=%fused_computation.15 | custom fusion | flops 196608 | bytes 395266 | tf_op jit(solution)/shard_map/scatter | solution.py:145
  9.8 1.5 %collective-permute-start.7 = (bf16[256,128]{1,0:T(8,128)(2,1)S(1)}, bf16[256,128]{1,0:T(8,128)(2,1)S(1)}, u32[]{:S(2)}, u32[]{:S(2)}) collective-permute-start(bf16[256,128]{1,0:T(8,128)(2,1)S(1)} %get-tuple-element.7), channel_id=1, source_target_pairs={{0,8},{8,16},{16,24},{24,0},{1,9},{9,17},{17,25},{25,1},{2,10},{10... | collective-permute-start | bytes 196616 | tf_op jit(solution)/shard_map/ppermute | solution.py:120
  11.4 0.5 %collective-permute-start.8 = (bf16[256,128]{1,0:T(8,128)(2,1)S(1)}, bf16[256,128]{1,0:T(8,128)(2,1)S(1)}, u32[]{:S(2)}, u32[]{:S(2)}) collective-permute-start(bf16[256,128]{1,0:T(8,128)(2,1)S(1)} %get-tuple-element.6), channel_id=1, source_target_pairs={{0,16},{8,24},{16,0},{24,8},{1,17},{9,25},{17,1},{25,9},{2,18},{10... | collective-permute-start | bytes 196616 | tf_op jit(solution)/shard_map/ppermute | solution.py:120
  11.9 1.5 %collective-permute-start.9 = (bf16[256,128]{1,0:T(8,128)(2,1)S(1)}, bf16[256,128]{1,0:T(8,128)(2,1)S(1)}, u32[]{:S(2)}, u32[]{:S(2)}) collective-permute-start(bf16[256,128]{1,0:T(8,128)(2,1)S(1)} %get-tuple-element.5), channel_id=1, source_target_pairs={{0,24},{8,0},{16,8},{24,16},{1,25},{9,1},{17,9},{25,17},{2,26},{10... | collective-permute-start | bytes 196616 | tf_op jit(solution)/shard_map/ppermute | solution.py:120
  13.4 1.0 %constant_dynamic-update-slice_fusion.7 = bf16[8192,128]{1,0:T(8,128)(2,1)S(1)} fusion(bf16[1024,128]{1,0:T(8,128)(2,1)} %param.7), kind=kLoop, calls=%fused_computation.24 | loop fusion | bytes 524288
  14.4 0.0 collective-permute-done.7
  14.4 0.1 collective-permute-start.2
  14.5 1.3 %collective-permute-done.8 = bf16[256,128]{1,0:T(8,128)(2,1)S(1)} collective-permute-done((bf16[256,128]{1,0:T(8,128)(2,1)S(1)}, bf16[256,128]{1,0:T(8,128)(2,1)S(1)}, u32[]{:S(2)}, u32[]{:S(2)}) %collective-permute-start.8) | collective-permute-done | bytes 65568 | tf_op jit(solution)/shard_map/ppermute | solution.py:120
  15.8 0.0 collective-permute-start.3
  15.8 1.3 %collective-permute-done.9 = bf16[256,128]{1,0:T(8,128)(2,1)S(1)} collective-permute-done((bf16[256,128]{1,0:T(8,128)(2,1)S(1)}, bf16[256,128]{1,0:T(8,128)(2,1)S(1)}, u32[]{:S(2)}, u32[]{:S(2)}) %collective-permute-start.9) | collective-permute-done | bytes 65568 | tf_op jit(solution)/shard_map/ppermute | solution.py:120
  17.1 0.0 collective-permute-done
  17.1 0.1 collective-permute-start.4
  17.2 6.6 %collective-permute-done.1 = bf16[1024,128]{1,0:T(8,128)(2,1)S(1)} collective-permute-done((bf16[1024,128]{1,0:T(8,128)(2,1)}, bf16[1024,128]{1,0:T(8,128)(2,1)S(1)}, u32[]{:S(2)}, u32[]{:S(2)}) %collective-permute-start.1) | collective-permute-done | bytes 262176 | tf_op jit(solution)/shard_map/ppermute | solution.py:129
  23.8 0.0 collective-permute-start.5
  23.8 2.9 %collective-permute-done.2 = bf16[1024,128]{1,0:T(8,128)(2,1)S(1)} collective-permute-done((bf16[1024,128]{1,0:T(8,128)(2,1)}, bf16[1024,128]{1,0:T(8,128)(2,1)S(1)}, u32[]{:S(2)}, u32[]{:S(2)}) %collective-permute-start.2) | collective-permute-done | bytes 262176 | tf_op jit(solution)/shard_map/ppermute | solution.py:129
  26.7 0.0 collective-permute-start.6
  26.8 0.0 collective-permute-done.3
  26.9 0.0 collective-permute-done.4
  26.9 0.0 collective-permute-done.5
  27.0 1.3 %collective-permute-done.6 = bf16[1024,128]{1,0:T(8,128)(2,1)S(1)} collective-permute-done((bf16[1024,128]{1,0:T(8,128)(2,1)S(1)}, bf16[1024,128]{1,0:T(8,128)(2,1)S(1)}, u32[]{:S(2)}, u32[]{:S(2)}) %collective-permute-start.6) | collective-permute-done | bytes 262176 | tf_op jit(solution)/shard_map/ppermute | solution.py:131
  28.3 9.2 %shard_map.60 = bf16[768,128]{1,0:T(8,128)(2,1)S(1)} custom-call(bf16[768,128]{1,0:T(8,128)(2,1)S(1)} %pad_maximum_fusion.refs_0_, bf16[8192,128]{1,0:T(8,128)(2,1)S(1)} %constant_dynamic-update-slice_fusion.refs_1_), custom_call_target="tpu_custom_call" | custom-call | flops 3221225472 | bytes 2490368 | tf_op jit(solution)/shard_map/pallas_call | solution.py:92
  37.5 0.0 copy-start
  37.6 0.0 copy-start.1
  37.6 0.6 %collective-permute-start.10 = (bf16[256,128]{1,0:T(8,128)(2,1)S(1)}, bf16[256,128]{1,0:T(8,128)(2,1)S(1)}, u32[]{:S(2)}, u32[]{:S(2)}) collective-permute-start(bf16[256,128]{1,0:T(8,128)(2,1)S(1)} %get-tuple-element.8), channel_id=1, source_target_pairs={{0,24},{8,0},{16,8},{24,16},{1,25},{9,1},{17,9},{25,17},{2,26},{10... | collective-permute-start | bytes 196616 | tf_op jit(solution)/shard_map/ppermute | solution.py:120
  38.2 1.5 %collective-permute-start.11 = (bf16[256,128]{1,0:T(8,128)(2,1)S(1)}, bf16[256,128]{1,0:T(8,128)(2,1)S(1)}, u32[]{:S(2)}, u32[]{:S(2)}) collective-permute-start(bf16[256,128]{1,0:T(8,128)(2,1)S(1)} %get-tuple-element.10), channel_id=1, source_target_pairs={{0,16},{8,24},{16,0},{24,8},{1,17},{9,25},{17,1},{25,9},{2,18},{10... | collective-permute-start | bytes 196616 | tf_op jit(solution)/shard_map/ppermute | solution.py:120
  39.7 2.4 %collective-permute-start.12 = (bf16[256,128]{1,0:T(8,128)(2,1)S(1)}, bf16[256,128]{1,0:T(8,128)(2,1)S(1)}, u32[]{:S(2)}, u32[]{:S(2)}) collective-permute-start(bf16[256,128]{1,0:T(8,128)(2,1)S(1)} %get-tuple-element.9), channel_id=1, source_target_pairs={{0,8},{8,16},{16,24},{24,0},{1,9},{9,17},{17,25},{25,1},{2,10},{10... | collective-permute-start | bytes 196616 | tf_op jit(solution)/shard_map/ppermute | solution.py:120
  42.1 3.7 %shard_map.59 = bf16[256,128]{1,0:T(8,128)(2,1)S(1)} custom-call(bf16[256,128]{1,0:T(8,128)(2,1)S(1)} %get-tuple-element.4.refs_0_, bf16[8192,128]{1,0:T(8,128)(2,1)S(1)} %constant_dynamic-update-slice_fusion.refs_1_), custom_call_target="tpu_custom_call" | custom-call | flops 1073741824 | bytes 2228224 | tf_op jit(solution)/shard_map/pallas_call | solution.py:92
  45.8 0.0 collective-permute-done.10
  45.8 0.0 collective-permute-done.11
  45.8 0.0 collective-permute-done.12
  45.8 0.0 copy-done
  45.9 0.0 copy-done.1
  45.9 1.2 %subtract_convert_fusion = (bf16[512,128]{1,0:T(8,128)(2,1)}, bf16[512,128]{1,0:T(8,128)(2,1)}) fusion(f32[512]{0:T(512)S(1)} %copy-done.1, bf16[512,128]{1,0:T(8,128)(2,1)S(1)} %copy-done, bf16[256,128]{1,0:T(8,128)(2,1)S(1)} %collective-permute-done.12, bf16[256,128]{1,0:T(8,128)(2,1)S(1)} %collective-permute-done.11, ...), kind=kOutput, calls=%fused_computation.12 | convolution fusion | flops 136314880 | bytes 659456 | tf_op jit(solution)/shard_map/dot_general | solution.py:154
  (10 shorter events, 0.3 us)
Async XLA Ops:
  0.6 16.4 %collective-permute-start = (bf16[1024,128]{1,0:T(8,128)(2,1)}, bf16[1024,128]{1,0:T(8,128)(2,1)S(1)}, u32[]{:S(2)}, u32[]{:S(2)}) collective-permute-start(bf16[1024,128]{1,0:T(8,128)(2,1)} %param.7), channel_id=1, source_target_pairs={{0,4},{1,5},{2,6},{3,7},{4,0},{5,1},{6,2},{7,3},{8,12},{9,13},{10,... | collective-permute-start | bytes 786440 | tf_op jit(solution)/shard_map/ppermute | solution.py:129
  1.0 22.8 %collective-permute-start.1 = (bf16[1024,128]{1,0:T(8,128)(2,1)}, bf16[1024,128]{1,0:T(8,128)(2,1)S(1)}, u32[]{:S(2)}, u32[]{:S(2)}) collective-permute-start(bf16[1024,128]{1,0:T(8,128)(2,1)} %param.7), channel_id=1, source_target_pairs={{0,6},{1,7},{2,0},{3,1},{4,2},{5,3},{6,4},{7,5},{8,14},{9,15},{10,... | collective-permute-start | bytes 786440 | tf_op jit(solution)/shard_map/ppermute | solution.py:129
  9.8 4.6 %collective-permute-start.7 = (bf16[256,128]{1,0:T(8,128)(2,1)S(1)}, bf16[256,128]{1,0:T(8,128)(2,1)S(1)}, u32[]{:S(2)}, u32[]{:S(2)}) collective-permute-start(bf16[256,128]{1,0:T(8,128)(2,1)S(1)} %get-tuple-element.7), channel_id=1, source_target_pairs={{0,8},{8,16},{16,24},{24,0},{1,9},{9,17},{17,25},{25,1},{2,10},{10... | collective-permute-start | bytes 196616 | tf_op jit(solution)/shard_map/ppermute | solution.py:120
  11.4 4.4 %collective-permute-start.8 = (bf16[256,128]{1,0:T(8,128)(2,1)S(1)}, bf16[256,128]{1,0:T(8,128)(2,1)S(1)}, u32[]{:S(2)}, u32[]{:S(2)}) collective-permute-start(bf16[256,128]{1,0:T(8,128)(2,1)S(1)} %get-tuple-element.6), channel_id=1, source_target_pairs={{0,16},{8,24},{16,0},{24,8},{1,17},{9,25},{17,1},{25,9},{2,18},{10... | collective-permute-start | bytes 196616 | tf_op jit(solution)/shard_map/ppermute | solution.py:120
  11.9 5.2 %collective-permute-start.9 = (bf16[256,128]{1,0:T(8,128)(2,1)S(1)}, bf16[256,128]{1,0:T(8,128)(2,1)S(1)}, u32[]{:S(2)}, u32[]{:S(2)}) collective-permute-start(bf16[256,128]{1,0:T(8,128)(2,1)S(1)} %get-tuple-element.5), channel_id=1, source_target_pairs={{0,24},{8,0},{16,8},{24,16},{1,25},{9,1},{17,9},{25,17},{2,26},{10... | collective-permute-start | bytes 196616 | tf_op jit(solution)/shard_map/ppermute | solution.py:120
  14.4 12.3 %collective-permute-start.2 = (bf16[1024,128]{1,0:T(8,128)(2,1)}, bf16[1024,128]{1,0:T(8,128)(2,1)S(1)}, u32[]{:S(2)}, u32[]{:S(2)}) collective-permute-start(bf16[1024,128]{1,0:T(8,128)(2,1)} %param.7), channel_id=1, source_target_pairs={{0,2},{1,3},{2,4},{3,5},{4,6},{5,7},{6,0},{7,1},{8,10},{9,11},{10,... | collective-permute-start | bytes 786440 | tf_op jit(solution)/shard_map/ppermute | solution.py:129
  15.8 11.0 %collective-permute-start.3 = (bf16[1024,128]{1,0:T(8,128)(2,1)}, bf16[1024,128]{1,0:T(8,128)(2,1)S(1)}, u32[]{:S(2)}, u32[]{:S(2)}) collective-permute-start(bf16[1024,128]{1,0:T(8,128)(2,1)} %param.7), channel_id=1, source_target_pairs={{0,1},{1,0},{2,3},{3,2},{4,5},{5,4},{6,7},{7,6},{8,9},{9,8},{10,11... | collective-permute-start | bytes 786440 | tf_op jit(solution)/shard_map/ppermute | solution.py:131
  17.1 9.8 %collective-permute-start.4 = (bf16[1024,128]{1,0:T(8,128)(2,1)S(1)}, bf16[1024,128]{1,0:T(8,128)(2,1)S(1)}, u32[]{:S(2)}, u32[]{:S(2)}) collective-permute-start(bf16[1024,128]{1,0:T(8,128)(2,1)S(1)} %collective-permute-done), channel_id=1, source_target_pairs={{0,1},{1,0},{2,3},{3,2},{4,5},{5,4},{6,7},{7,6},{8,9},{9,8},{10,11... | collective-permute-start | bytes 786440 | tf_op jit(solution)/shard_map/ppermute | solution.py:131
  23.8 3.1 %collective-permute-start.5 = (bf16[1024,128]{1,0:T(8,128)(2,1)S(1)}, bf16[1024,128]{1,0:T(8,128)(2,1)S(1)}, u32[]{:S(2)}, u32[]{:S(2)}) collective-permute-start(bf16[1024,128]{1,0:T(8,128)(2,1)S(1)} %collective-permute-done.1), channel_id=1, source_target_pairs={{0,1},{1,0},{2,3},{3,2},{4,5},{5,4},{6,7},{7,6},{8,9},{9,8},{10,11... | collective-permute-start | bytes 786440 | tf_op jit(solution)/shard_map/ppermute | solution.py:131
  26.7 1.5 %collective-permute-start.6 = (bf16[1024,128]{1,0:T(8,128)(2,1)S(1)}, bf16[1024,128]{1,0:T(8,128)(2,1)S(1)}, u32[]{:S(2)}, u32[]{:S(2)}) collective-permute-start(bf16[1024,128]{1,0:T(8,128)(2,1)S(1)} %collective-permute-done.2), channel_id=1, source_target_pairs={{0,1},{1,0},{2,3},{3,2},{4,5},{5,4},{6,7},{7,6},{8,9},{9,8},{10,11... | collective-permute-start | bytes 786440 | tf_op jit(solution)/shard_map/ppermute | solution.py:131
  37.5 8.3 %copy-start = (bf16[512,128]{1,0:T(8,128)(2,1)S(1)}, bf16[512,128]{1,0:T(8,128)(2,1)}, u32[]{:S(2)}) copy-start(bf16[512,128]{1,0:T(8,128)(2,1)} %param.4) | copy-start | bytes 393220
  37.6 8.3 %copy-start.1 = (f32[512]{0:T(512)S(1)}, f32[512]{0:T(512)}, u32[]{:S(2)}) copy-start(f32[512]{0:T(512)} %param.5) | copy-start | bytes 6148
  37.6 8.2 %collective-permute-start.10 = (bf16[256,128]{1,0:T(8,128)(2,1)S(1)}, bf16[256,128]{1,0:T(8,128)(2,1)S(1)}, u32[]{:S(2)}, u32[]{:S(2)}) collective-permute-start(bf16[256,128]{1,0:T(8,128)(2,1)S(1)} %get-tuple-element.8), channel_id=1, source_target_pairs={{0,24},{8,0},{16,8},{24,16},{1,25},{9,1},{17,9},{25,17},{2,26},{10... | collective-permute-start | bytes 196616 | tf_op jit(solution)/shard_map/ppermute | solution.py:120
  38.2 7.6 %collective-permute-start.11 = (bf16[256,128]{1,0:T(8,128)(2,1)S(1)}, bf16[256,128]{1,0:T(8,128)(2,1)S(1)}, u32[]{:S(2)}, u32[]{:S(2)}) collective-permute-start(bf16[256,128]{1,0:T(8,128)(2,1)S(1)} %get-tuple-element.10), channel_id=1, source_target_pairs={{0,16},{8,24},{16,0},{24,8},{1,17},{9,25},{17,1},{25,9},{2,18},{10... | collective-permute-start | bytes 196616 | tf_op jit(solution)/shard_map/ppermute | solution.py:120
  39.7 6.1 %collective-permute-start.12 = (bf16[256,128]{1,0:T(8,128)(2,1)S(1)}, bf16[256,128]{1,0:T(8,128)(2,1)S(1)}, u32[]{:S(2)}, u32[]{:S(2)}) collective-permute-start(bf16[256,128]{1,0:T(8,128)(2,1)S(1)} %get-tuple-element.9), channel_id=1, source_target_pairs={{0,8},{8,16},{16,24},{24,0},{1,9},{9,17},{17,25},{25,1},{2,10},{10... | collective-permute-start | bytes 196616 | tf_op jit(solution)/shard_map/ppermute | solution.py:120

commit v6 on v5

--- a/solution.py
+++ b/solution.py
@@ -149,9 +149,10 @@
     first = soft_part(jnp.concatenate(arrived[1:], axis=0), part, final=True)
     ret = {d: _shift(first[(d - 1) * cap:d * cap], "cell", loops, -d) for d in range(1, loops)}
     ret[0] = soft_part(arrived[0], part, final=True)
-    back = jnp.concatenate([ret[d] for d in range(loops)], axis=0)
-    pick = slots[:, None] == jnp.arange(back.shape[0], dtype=jnp.int32)[None, :]
-    mine = jnp.dot(pick.astype(jnp.bfloat16), back, preferred_element_type=jnp.float32)
+    pick = (slots[:, None] == jnp.arange(loops * cap, dtype=jnp.int32)[None, :]).astype(jnp.bfloat16)
+    own = jnp.dot(pick[:, :cap], ret[0], preferred_element_type=jnp.float32)
+    remote = jnp.concatenate([ret[d] for d in range(1, loops)], axis=0)
+    mine = own + jnp.dot(pick[:, cap:], remote, preferred_element_type=jnp.float32)
     mine = mine.astype(jnp.bfloat16)
     residual = (dequant.astype(jnp.float32) - mine.astype(jnp.float32)).astype(jnp.bfloat16)
     return (mine, residual)

time: 47.3 us -> 47.4 us (level)
    dot_general x1 -> x2, matrix products: 1.22 us -> 1.32 us  [the longest x1 0.93 us: _local(): own = jnp.dot(pick[:, :cap], ret[0], preferred_element_type=jnp.float32)]
  transfers between devices with their start and end apart: 13 -> 13, of which waited for: 5 -> 5; matrix products, arithmetic and copies ran while one was open for 15% -> 16% of each run, Pallas kernels for 8% -> 8%
where the time goes in v6:
time: 47.4 us; the launch traced here: 47.2 us
  waiting for transfers between devices  13 us (27%)
  Pallas kernels  12.9 us (27%)
  starting transfers between devices  11.4 us (24%)
  other arithmetic  6.21 us (13%)
  local copies, waits for them, and re-layouts  1.48 us (3%)
  matrix products  1.32 us (3%)
  between operations  0.84 us (2%)
    pallas_call x2, Pallas kernels, soft_part(): pl.pallas_call(functools.partial(_soft_kernel, chunk=chunk, beta=1.0 / ma...  12.9 us
    ppermute x3, waiting for transfers between devices, _gather_partition(): pieces.append(lax.ppermute(centroids, 'blk', pairs))  9.51 us
    ppermute x6, starting transfers between devices, _shift(): return lax.ppermute(x, axis, [(i, (i + d) % n) for i in range(n)])  8.1 us
    ppermute x3, starting transfers between devices, _gather_partition(): pieces.append(lax.ppermute(centroids, 'blk', pairs))  3.16 us
    scatter x1, other arithmetic, _local(): jnp.zeros((loops * cap, width), jnp.bfloat16).at[slots].set(dequant)  2.28 us
    ppermute x6, waiting for transfers between devices, _shift(): return lax.ppermute(x, axis, [(i, (i + d) % n) for i in range(n)])  2.21 us
    another operation x2, other arithmetic  1.39 us
    ppermute x4, waiting for transfers between devices, _gather_partition(): swapped = [lax.ppermute(p, 'blk', swap) for p in pieces]  1.32 us
  transfers between devices with their start and end apart: 13, of which 5 were waited for; matrix products, arithmetic and copies ran while one was open for 16% of the time, Pallas kernels for 8%

profile of v6, /device:TPU:18, one launch (start us, length us, event | category | flops | bytes accessed | tf_op | source)
XLA Modules:
  0.0 47.2 jit_solution(998485368063258189)
XLA Ops:
  0.6 0.4 collective-permute-start
  1.0 2.7 %collective-permute-start.1 = (bf16[1024,128]{1,0:T(8,128)(2,1)}, bf16[1024,128]{1,0:T(8,128)(2,1)S(1)}, u32[]{:S(2)}, u32[]{:S(2)}) collective-permute-start(bf16[1024,128]{1,0:T(8,128)(2,1)} %param.7), channel_id=1, source_target_pairs={{0,6},{1,7},{2,0},{3,1},{4,2},{5,3},{6,4},{7,5},{8,14},{9,15},{10,... | collective-permute-start | bytes 786440 | tf_op jit(solution)/shard_map/ppermute | solution.py:129
  3.7 0.7 %fusion.13 = s32[4,4,128]{2,1,0:T(4,128)S(1)} fusion(s32[4,128]{1,0:T(4,128)} %bitcast.17), kind=kLoop, calls=%fused_computation.32 | loop fusion | flops 4096 | bytes 10240 | tf_op jit(solution)/shard_map/convert_element_type | solution.py:142
  4.4 1.2 %reduce-window.6 = s32[4,4,128]{2,1,0:T(4,128)S(1)} reduce-window(s32[4,4,128]{2,1,0:T(4,128)S(1)} %fusion.13, s32[]{:T(128)} %constant.28.clone.1), window={size=1x1x128 pad=0_0x0_0x127_0}, to_apply=%region_0.0 | reduce-window | flops 260096 | bytes 16388 | tf_op jit(solution)/shard_map/reduce-window
  5.6 0.2 slice_reduce_fusion
  5.8 0.2 reduce-window.9
  6.0 0.1 add_bitcast_fusion
  6.1 0.7 %fusion.12 = s32[512]{0:T(512)S(1)} fusion(s32[1,4,4,128]{3,2,1,0:T(4,128)S(1)} %add_bitcast_fusion, s32[512]{0:T(512)} %param.6), kind=kLoop, calls=%fused_computation.27 | loop fusion | flops 5632 | bytes 12288 | tf_op jit(solution)/shard_map/reduce_sum | solution.py:143
  6.8 0.7 %compare_select_fusion = (s32[512]{0:T(512)S(1)}, s32[512]{0:T(512)S(1)}) fusion(s32[512]{0:T(512)S(1)} %fusion.12, s32[512]{0:T(512)} %param.6, s32[]{:T(128)S(6)} %axis_index.15), kind=kLoop, calls=%fused_computation.33 | loop fusion | flops 9216 | bytes 8196 | tf_op jit(solution)/shard_map/select_n | solution.py:145
  7.5 2.3 %scatter_custom_fusion = bf16[1024,128]{1,0:T(8,128)(2,1)S(1)} fusion(s32[512]{0:T(512)S(1)} %get-tuple-element.2, bf16[]{:T(256)} %constant.33.clone.1, bf16[512,128]{1,0:T(8,128)(2,1)} %param.4, f32[512]{0:T(512)} %param.5), kind=kCustom, calls=%fused_computation.15 | custom fusion | flops 196608 | bytes 395266 | tf_op jit(solution)/shard_map/scatter | solution.py:145
  9.8 1.5 %collective-permute-start.7 = (bf16[256,128]{1,0:T(8,128)(2,1)S(1)}, bf16[256,128]{1,0:T(8,128)(2,1)S(1)}, u32[]{:S(2)}, u32[]{:S(2)}) collective-permute-start(bf16[256,128]{1,0:T(8,128)(2,1)S(1)} %get-tuple-element.7), channel_id=1, source_target_pairs={{0,8},{8,16},{16,24},{24,0},{1,9},{9,17},{17,25},{25,1},{2,10},{10... | collective-permute-start | bytes 196616 | tf_op jit(solution)/shard_map/ppermute | solution.py:120
  11.4 0.5 %collective-permute-start.8 = (bf16[256,128]{1,0:T(8,128)(2,1)S(1)}, bf16[256,128]{1,0:T(8,128)(2,1)S(1)}, u32[]{:S(2)}, u32[]{:S(2)}) collective-permute-start(bf16[256,128]{1,0:T(8,128)(2,1)S(1)} %get-tuple-element.6), channel_id=1, source_target_pairs={{0,16},{8,24},{16,0},{24,8},{1,17},{9,25},{17,1},{25,9},{2,18},{10... | collective-permute-start | bytes 196616 | tf_op jit(solution)/shard_map/ppermute | solution.py:120
  11.9 1.5 %collective-permute-start.9 = (bf16[256,128]{1,0:T(8,128)(2,1)S(1)}, bf16[256,128]{1,0:T(8,128)(2,1)S(1)}, u32[]{:S(2)}, u32[]{:S(2)}) collective-permute-start(bf16[256,128]{1,0:T(8,128)(2,1)S(1)} %get-tuple-element.5), channel_id=1, source_target_pairs={{0,24},{8,0},{16,8},{24,16},{1,25},{9,1},{17,9},{25,17},{2,26},{10... | collective-permute-start | bytes 196616 | tf_op jit(solution)/shard_map/ppermute | solution.py:120
  13.4 0.4 iota_compare_fusion
  13.8 1.0 %constant_dynamic-update-slice_fusion.7 = bf16[8192,128]{1,0:T(8,128)(2,1)S(1)} fusion(bf16[1024,128]{1,0:T(8,128)(2,1)} %param.7), kind=kLoop, calls=%fused_computation.24 | loop fusion | bytes 524288
  14.8 0.0 collective-permute-done.7
  14.8 0.1 collective-permute-start.2
  14.8 0.9 %collective-permute-done.8 = bf16[256,128]{1,0:T(8,128)(2,1)S(1)} collective-permute-done((bf16[256,128]{1,0:T(8,128)(2,1)S(1)}, bf16[256,128]{1,0:T(8,128)(2,1)S(1)}, u32[]{:S(2)}, u32[]{:S(2)}) %collective-permute-start.8) | collective-permute-done | bytes 65568 | tf_op jit(solution)/shard_map/ppermute | solution.py:120
  15.8 0.0 collective-permute-start.3
  15.8 1.3 %collective-permute-done.9 = bf16[256,128]{1,0:T(8,128)(2,1)S(1)} collective-permute-done((bf16[256,128]{1,0:T(8,128)(2,1)S(1)}, bf16[256,128]{1,0:T(8,128)(2,1)S(1)}, u32[]{:S(2)}, u32[]{:S(2)}) %collective-permute-start.9) | collective-permute-done | bytes 65568 | tf_op jit(solution)/shard_map/ppermute | solution.py:120
  17.1 0.0 collective-permute-done
  17.1 0.1 collective-permute-start.4
  17.2 6.6 %collective-permute-done.1 = bf16[1024,128]{1,0:T(8,128)(2,1)S(1)} collective-permute-done((bf16[1024,128]{1,0:T(8,128)(2,1)}, bf16[1024,128]{1,0:T(8,128)(2,1)S(1)}, u32[]{:S(2)}, u32[]{:S(2)}) %collective-permute-start.1) | collective-permute-done | bytes 262176 | tf_op jit(solution)/shard_map/ppermute | solution.py:129
  23.8 0.0 collective-permute-start.5
  23.8 2.9 %collective-permute-done.2 = bf16[1024,128]{1,0:T(8,128)(2,1)S(1)} collective-permute-done((bf16[1024,128]{1,0:T(8,128)(2,1)}, bf16[1024,128]{1,0:T(8,128)(2,1)S(1)}, u32[]{:S(2)}, u32[]{:S(2)}) %collective-permute-start.2) | collective-permute-done | bytes 262176 | tf_op jit(solution)/shard_map/ppermute | solution.py:129
  26.7 0.0 collective-permute-start.6
  26.8 0.0 collective-permute-done.3
  26.9 0.0 collective-permute-done.4
  26.9 0.0 collective-permute-done.5
  27.0 1.3 %collective-permute-done.6 = bf16[1024,128]{1,0:T(8,128)(2,1)S(1)} collective-permute-done((bf16[1024,128]{1,0:T(8,128)(2,1)S(1)}, bf16[1024,128]{1,0:T(8,128)(2,1)S(1)}, u32[]{:S(2)}, u32[]{:S(2)}) %collective-permute-start.6) | collective-permute-done | bytes 262176 | tf_op jit(solution)/shard_map/ppermute | solution.py:131
  28.3 9.2 %shard_map.60 = bf16[768,128]{1,0:T(8,128)(2,1)S(1)} custom-call(bf16[768,128]{1,0:T(8,128)(2,1)S(1)} %pad_maximum_fusion.refs_0_, bf16[8192,128]{1,0:T(8,128)(2,1)S(1)} %constant_dynamic-update-slice_fusion.refs_1_), custom_call_target="tpu_custom_call" | custom-call | flops 3221225472 | bytes 2490368 | tf_op jit(solution)/shard_map/pallas_call | solution.py:92
  37.6 0.6 %collective-permute-start.10 = (bf16[256,128]{1,0:T(8,128)(2,1)S(1)}, bf16[256,128]{1,0:T(8,128)(2,1)S(1)}, u32[]{:S(2)}, u32[]{:S(2)}) collective-permute-start(bf16[256,128]{1,0:T(8,128)(2,1)S(1)} %get-tuple-element.8), channel_id=1, source_target_pairs={{0,24},{8,0},{16,8},{24,16},{1,25},{9,1},{17,9},{25,17},{2,26},{10... | collective-permute-start | bytes 196616 | tf_op jit(solution)/shard_map/ppermute | solution.py:120
  38.2 1.5 %collective-permute-start.11 = (bf16[256,128]{1,0:T(8,128)(2,1)S(1)}, bf16[256,128]{1,0:T(8,128)(2,1)S(1)}, u32[]{:S(2)}, u32[]{:S(2)}) collective-permute-start(bf16[256,128]{1,0:T(8,128)(2,1)S(1)} %get-tuple-element.10), channel_id=1, source_target_pairs={{0,16},{8,24},{16,0},{24,8},{1,17},{9,25},{17,1},{25,9},{2,18},{10... | collective-permute-start | bytes 196616 | tf_op jit(solution)/shard_map/ppermute | solution.py:120
  39.7 2.4 %collective-permute-start.12 = (bf16[256,128]{1,0:T(8,128)(2,1)S(1)}, bf16[256,128]{1,0:T(8,128)(2,1)S(1)}, u32[]{:S(2)}, u32[]{:S(2)}) collective-permute-start(bf16[256,128]{1,0:T(8,128)(2,1)S(1)} %get-tuple-element.9), channel_id=1, source_target_pairs={{0,8},{8,16},{16,24},{24,0},{1,9},{9,17},{17,25},{25,1},{2,10},{10... | collective-permute-start | bytes 196616 | tf_op jit(solution)/shard_map/ppermute | solution.py:120
  42.1 0.0 copy-start
  42.1 0.0 copy-start.1
  42.1 3.7 %shard_map.59 = bf16[256,128]{1,0:T(8,128)(2,1)S(1)} custom-call(bf16[256,128]{1,0:T(8,128)(2,1)S(1)} %get-tuple-element.4.refs_0_, bf16[8192,128]{1,0:T(8,128)(2,1)S(1)} %constant_dynamic-update-slice_fusion.refs_1_), custom_call_target="tpu_custom_call" | custom-call | flops 1073741824 | bytes 2228224 | tf_op jit(solution)/shard_map/pallas_call | solution.py:92
  45.8 0.0 collective-permute-done.10
  45.8 0.0 collective-permute-done.11
  45.8 0.0 collective-permute-done.12
  45.8 0.4 fusion
  46.2 0.0 copy-done
  46.2 0.0 copy-done.1
  46.2 0.9 %subtract_convert_fusion = (bf16[512,128]{1,0:T(8,128)(2,1)}, bf16[512,128]{1,0:T(8,128)(2,1)}) fusion(f32[512]{0:T(512)S(1)} %copy-done.1, bf16[512,128]{1,0:T(8,128)(2,1)S(1)} %copy-done, f32[512,128]{1,0:T(8,128)S(1)} %fusion, bf16[256,128]{1,0:T(8,128)(2,1)S(1)} %shard_map.59, pred[512,1024]{1,0:T(32,128)(4,1)S(1)} %iota_compare_fusion), kind=kOutput, calls=%fused_computation.7 | convolution fusion | flops 34144256 | bytes 854016 | tf_op jit(solution)/shard_map/dot_general | solution.py:153
  (10 shorter events, 0.3 us)
Async XLA Ops:
  0.6 16.4 %collective-permute-start = (bf16[1024,128]{1,0:T(8,128)(2,1)}, bf16[1024,128]{1,0:T(8,128)(2,1)S(1)}, u32[]{:S(2)}, u32[]{:S(2)}) collective-permute-start(bf16[1024,128]{1,0:T(8,128)(2,1)} %param.7), channel_id=1, source_target_pairs={{0,4},{1,5},{2,6},{3,7},{4,0},{5,1},{6,2},{7,3},{8,12},{9,13},{10,... | collective-permute-start | bytes 786440 | tf_op jit(solution)/shard_map/ppermute | solution.py:129
  1.0 22.8 %collective-permute-start.1 = (bf16[1024,128]{1,0:T(8,128)(2,1)}, bf16[1024,128]{1,0:T(8,128)(2,1)S(1)}, u32[]{:S(2)}, u32[]{:S(2)}) collective-permute-start(bf16[1024,128]{1,0:T(8,128)(2,1)} %param.7), channel_id=1, source_target_pairs={{0,6},{1,7},{2,0},{3,1},{4,2},{5,3},{6,4},{7,5},{8,14},{9,15},{10,... | collective-permute-start | bytes 786440 | tf_op jit(solution)/shard_map/ppermute | solution.py:129
  9.8 4.9 %collective-permute-start.7 = (bf16[256,128]{1,0:T(8,128)(2,1)S(1)}, bf16[256,128]{1,0:T(8,128)(2,1)S(1)}, u32[]{:S(2)}, u32[]{:S(2)}) collective-permute-start(bf16[256,128]{1,0:T(8,128)(2,1)S(1)} %get-tuple-element.7), channel_id=1, source_target_pairs={{0,8},{8,16},{16,24},{24,0},{1,9},{9,17},{17,25},{25,1},{2,10},{10... | collective-permute-start | bytes 196616 | tf_op jit(solution)/shard_map/ppermute | solution.py:120
  11.4 4.4 %collective-permute-start.8 = (bf16[256,128]{1,0:T(8,128)(2,1)S(1)}, bf16[256,128]{1,0:T(8,128)(2,1)S(1)}, u32[]{:S(2)}, u32[]{:S(2)}) collective-permute-start(bf16[256,128]{1,0:T(8,128)(2,1)S(1)} %get-tuple-element.6), channel_id=1, source_target_pairs={{0,16},{8,24},{16,0},{24,8},{1,17},{9,25},{17,1},{25,9},{2,18},{10... | collective-permute-start | bytes 196616 | tf_op jit(solution)/shard_map/ppermute | solution.py:120
  11.9 5.2 %collective-permute-start.9 = (bf16[256,128]{1,0:T(8,128)(2,1)S(1)}, bf16[256,128]{1,0:T(8,128)(2,1)S(1)}, u32[]{:S(2)}, u32[]{:S(2)}) collective-permute-start(bf16[256,128]{1,0:T(8,128)(2,1)S(1)} %get-tuple-element.5), channel_id=1, source_target_pairs={{0,24},{8,0},{16,8},{24,16},{1,25},{9,1},{17,9},{25,17},{2,26},{10... | collective-permute-start | bytes 196616 | tf_op jit(solution)/shard_map/ppermute | solution.py:120
  14.8 12.0 %collective-permute-start.2 = (bf16[1024,128]{1,0:T(8,128)(2,1)}, bf16[1024,128]{1,0:T(8,128)(2,1)S(1)}, u32[]{:S(2)}, u32[]{:S(2)}) collective-permute-start(bf16[1024,128]{1,0:T(8,128)(2,1)} %param.7), channel_id=1, source_target_pairs={{0,2},{1,3},{2,4},{3,5},{4,6},{5,7},{6,0},{7,1},{8,10},{9,11},{10,... | collective-permute-start | bytes 786440 | tf_op jit(solution)/shard_map/ppermute | solution.py:129
  15.8 11.0 %collective-permute-start.3 = (bf16[1024,128]{1,0:T(8,128)(2,1)}, bf16[1024,128]{1,0:T(8,128)(2,1)S(1)}, u32[]{:S(2)}, u32[]{:S(2)}) collective-permute-start(bf16[1024,128]{1,0:T(8,128)(2,1)} %param.7), channel_id=1, source_target_pairs={{0,1},{1,0},{2,3},{3,2},{4,5},{5,4},{6,7},{7,6},{8,9},{9,8},{10,11... | collective-permute-start | bytes 786440 | tf_op jit(solution)/shard_map/ppermute | solution.py:131
  17.1 9.8 %collective-permute-start.4 = (bf16[1024,128]{1,0:T(8,128)(2,1)S(1)}, bf16[1024,128]{1,0:T(8,128)(2,1)S(1)}, u32[]{:S(2)}, u32[]{:S(2)}) collective-permute-start(bf16[1024,128]{1,0:T(8,128)(2,1)S(1)} %collective-permute-done), channel_id=1, source_target_pairs={{0,1},{1,0},{2,3},{3,2},{4,5},{5,4},{6,7},{7,6},{8,9},{9,8},{10,11... | collective-permute-start | bytes 786440 | tf_op jit(solution)/shard_map/ppermute | solution.py:131
  23.8 3.1 %collective-permute-start.5 = (bf16[1024,128]{1,0:T(8,128)(2,1)S(1)}, bf16[1024,128]{1,0:T(8,128)(2,1)S(1)}, u32[]{:S(2)}, u32[]{:S(2)}) collective-permute-start(bf16[1024,128]{1,0:T(8,128)(2,1)S(1)} %collective-permute-done.1), channel_id=1, source_target_pairs={{0,1},{1,0},{2,3},{3,2},{4,5},{5,4},{6,7},{7,6},{8,9},{9,8},{10,11... | collective-permute-start | bytes 786440 | tf_op jit(solution)/shard_map/ppermute | solution.py:131
  26.7 1.5 %collective-permute-start.6 = (bf16[1024,128]{1,0:T(8,128)(2,1)S(1)}, bf16[1024,128]{1,0:T(8,128)(2,1)S(1)}, u32[]{:S(2)}, u32[]{:S(2)}) collective-permute-start(bf16[1024,128]{1,0:T(8,128)(2,1)S(1)} %collective-permute-done.2), channel_id=1, source_target_pairs={{0,1},{1,0},{2,3},{3,2},{4,5},{5,4},{6,7},{7,6},{8,9},{9,8},{10,11... | collective-permute-start | bytes 786440 | tf_op jit(solution)/shard_map/ppermute | solution.py:131
  37.6 8.2 %collective-permute-start.10 = (bf16[256,128]{1,0:T(8,128)(2,1)S(1)}, bf16[256,128]{1,0:T(8,128)(2,1)S(1)}, u32[]{:S(2)}, u32[]{:S(2)}) collective-permute-start(bf16[256,128]{1,0:T(8,128)(2,1)S(1)} %get-tuple-element.8), channel_id=1, source_target_pairs={{0,24},{8,0},{16,8},{24,16},{1,25},{9,1},{17,9},{25,17},{2,26},{10... | collective-permute-start | bytes 196616 | tf_op jit(solution)/shard_map/ppermute | solution.py:120
  38.2 7.6 %collective-permute-start.11 = (bf16[256,128]{1,0:T(8,128)(2,1)S(1)}, bf16[256,128]{1,0:T(8,128)(2,1)S(1)}, u32[]{:S(2)}, u32[]{:S(2)}) collective-permute-start(bf16[256,128]{1,0:T(8,128)(2,1)S(1)} %get-tuple-element.10), channel_id=1, source_target_pairs={{0,16},{8,24},{16,0},{24,8},{1,17},{9,25},{17,1},{25,9},{2,18},{10... | collective-permute-start | bytes 196616 | tf_op jit(solution)/shard_map/ppermute | solution.py:120
  39.7 6.1 %collective-permute-start.12 = (bf16[256,128]{1,0:T(8,128)(2,1)S(1)}, bf16[256,128]{1,0:T(8,128)(2,1)S(1)}, u32[]{:S(2)}, u32[]{:S(2)}) collective-permute-start(bf16[256,128]{1,0:T(8,128)(2,1)S(1)} %get-tuple-element.9), channel_id=1, source_target_pairs={{0,8},{8,16},{16,24},{24,0},{1,9},{9,17},{17,25},{25,1},{2,10},{10... | collective-permute-start | bytes 196616 | tf_op jit(solution)/shard_map/ppermute | solution.py:120
  42.1 4.1 %copy-start = (bf16[512,128]{1,0:T(8,128)(2,1)S(1)}, bf16[512,128]{1,0:T(8,128)(2,1)}, u32[]{:S(2)}) copy-start(bf16[512,128]{1,0:T(8,128)(2,1)} %param.4) | copy-start | bytes 393220
  42.1 4.2 %copy-start.1 = (f32[512]{0:T(512)S(1)}, f32[512]{0:T(512)}, u32[]{:S(2)}) copy-start(f32[512]{0:T(512)} %param.5) | copy-start | bytes 6148
